TPU v7x, 512 devices: a whole 4x8x8 slice. The times are simulated.
512 devices in a mesh: grp: 64 (over x, y, z_lo), mem: 8 (over z_hi, core).
Axes of the slice: x: 4, y: 8, z: 8 (z_hi: 4, z_lo: 2; z = z_hi * 2 + z_lo), core: 2. Of those that a mesh axis runs over, the one named last changes fastest.
Arguments:
- raw_traces: float32 [4096, 6030], P(('grp', 'mem')), may hold values from -6 to 6
Outputs:
- correlations: bfloat16 [4096, 512, 401], P(('grp', 'mem'))
All inputs are finite; a program needn't handle non-finite values.
Results may differ from a plain program's by a relative error of at most 0.0063.
Values may be sent and summed in bfloat16 or wider, within the bound.
No kernel may reach another device: no remote copies, remote signals or barrier semaphores. Data moves between devices by JAX's collectives and lax.ppermute only.
A program may use at most 64 MiB of HBM per device.

v0:
```python
import math

import jax
import jax.numpy as jnp
from jax import lax
from jax.sharding import PartitionSpec as P

WINDOWS = 2
WLEN = 1500
NFREQ = 384
TAPS = 32
MAXLAG = 200


def lowpass(taps):
    k = jnp.arange(taps).astype(jnp.float32)
    centre = (taps - 1) / 2.0
    window = 0.5 - 0.5 * jnp.cos(2.0 * math.pi * (k + 0.5) / taps)
    return 0.5 * jnp.sinc((k - centre) * 0.5) * window


def forward_table(wlen, nfreq):
    times = jnp.arange(wlen)
    bins = jnp.arange(1, nfreq + 1)
    phase = times[:, None] * bins[None, :] % wlen
    angle = 2.0 * math.pi * phase.astype(jnp.float32) / wlen
    return jnp.concatenate([jnp.cos(angle), -jnp.sin(angle)], axis=1)


def inverse_table(wlen, nfreq, maxlag):
    bins = jnp.arange(1, nfreq + 1)
    shifts = jnp.arange(2 * maxlag + 1) - maxlag
    phase = jnp.mod(bins[:, None] * shifts[None, :], wlen)
    angle = 2.0 * math.pi * phase.astype(jnp.float32) / wlen
    return jnp.concatenate([jnp.cos(angle), -jnp.sin(angle)], axis=0).astype(jnp.bfloat16)


def whiten(raw_traces):
    count = raw_traces.shape[0]
    total = WINDOWS * WLEN
    filt = lowpass(TAPS)
    decimated = jnp.zeros((count, total), jnp.float32)
    for k in range(TAPS):
        piece = lax.slice(raw_traces, (0, k), (count, k + 2 * total - 1), (1, 2))
        decimated = decimated + filt[k] * piece
    frames = decimated.reshape(count * WINDOWS, WLEN)
    spec = jnp.dot(
        frames,
        forward_table(WLEN, NFREQ),
        precision=lax.Precision.HIGHEST,
        preferred_element_type=jnp.float32,
    )
    spec_re = spec[:, :NFREQ]
    spec_im = spec[:, NFREQ:]
    power = spec_re * spec_re + spec_im * spec_im
    level = 0.01 * jnp.mean(power, axis=1, keepdims=True)
    factor = 1.0 / jnp.sqrt(power + level + 1e-06)
    white = jnp.concatenate([spec_re * factor, spec_im * factor], axis=1)
    return white.astype(jnp.bfloat16).reshape(count, WINDOWS, 2 * NFREQ)


def on_device(raw_traces):
    white = whiten(raw_traces)
    count = white.shape[0]
    recv = white.astype(jnp.float32)
    recv_re = recv[:, :, :NFREQ]
    recv_im = recv[:, :, NFREQ:]
    table = inverse_table(WLEN, NFREQ, MAXLAG)
    lag_count = table.shape[1]
    scale = 1.0 / math.sqrt(WINDOWS * NFREQ)
    own_source = white[:1]
    panel = lax.all_gather(own_source, "mem", axis=0, tiled=True)
    piece = lax.all_gather(panel, "grp", axis=0, tiled=True)
    src = piece.astype(jnp.float32)
    src_re = src[:, :, :NFREQ]
    src_im = src[:, :, NFREQ:]
    cross_re = jnp.einsum("iwk,jwk->ijk", recv_re, src_re) + jnp.einsum(
        "iwk,jwk->ijk", recv_im, src_im
    )
    cross_im = jnp.einsum("iwk,jwk->ijk", recv_im, src_re) - jnp.einsum(
        "iwk,jwk->ijk", recv_re, src_im
    )
    cross = jnp.concatenate([cross_re, cross_im], axis=2).astype(jnp.bfloat16)
    width = piece.shape[0]
    flat = cross.reshape(count * width, 2 * NFREQ)
    corr = (jnp.dot(flat, table, preferred_element_type=jnp.float32) * scale).astype(jnp.bfloat16)
    return corr.reshape(count, width, lag_count)


def solution(mesh):
    return jax.shard_map(
        on_device,
        mesh=mesh,
        in_specs=(P(("grp", "mem"), None),),
        out_specs=P(("grp", "mem"), None, None),
        check_vma=False,
    )
```

profile of v0, /device:TPU:8, one launch (start us, length us, event | category | flops | bytes accessed | tf_op | source)
XLA Modules:
  0.0 507.8 jit_solution(8682816553093003616)
XLA Ops:
  8.0 4.1 slice.213
  12.2 4.1 slice.215
  16.3 4.1 slice.217
  20.4 4.1 slice.219
  24.6 4.3 slice.221
  28.9 4.1 slice.223
  33.0 4.1 slice.225
  37.2 4.1 slice.227
  41.3 4.1 slice.229
  45.5 4.3 slice.231
  49.8 4.1 slice.233
  54.0 4.1 slice.235
  58.1 4.1 slice.237
  62.3 4.1 slice.239
  66.4 4.5 slice.241
  70.9 4.1 slice.243
  75.1 3.2 slice.245
  78.3 3.2 slice.247
  81.5 3.4 slice.249
  84.9 3.2 slice.251
  88.1 3.2 slice.253
  91.4 3.2 slice.255
  94.6 3.2 slice.257
  97.8 3.4 slice.259
  101.2 3.2 slice.261
  104.4 3.2 slice.263
  107.7 3.2 slice.265
  110.9 3.2 slice.267
  114.1 3.6 slice.269
  117.7 3.2 slice.271
  120.9 3.2 slice.273
  124.1 3.2 slice.275
  127.4 20.3 %multiply_add_fusion = f32[8,3000]{1,0:T(8,128)S(1)} fusion(f32[8,3000]{1,0:T(8,128)S(1)} %slice.275, f32[8,3000]{1,0:T(8,128)S(1)} %slice.273, f32[8,3000]{1,0:T(8,128)S(1)} %slice.271, f32[8,3000]{1,0:T(8,128)S(1)} %slice.269, f32[8,3000]{1,0:T(8,128)S(1)} %slice.267, f32[8,3000]{1,0:T(8,128)S(1)} %slice.265, f32[8,3000]{1,0:T(8,128)S(1)} %slice.263, ...), kind=kLoop, calls=%fused_computation.33 | loop fusion | flops 1512000 | bytes 3168128 | tf_op jit(solution)/shard_map/add | solution.py:45
  147.8 9.5 %fusion.14 = (f32[1500,384]{1,0:T(8,128)S(1)}, f32[1500,384]{1,0:T(8,128)S(1)}) fusion(s32[384]{0:T(512)S(1)} %iota_add_fusion.1), kind=kLoop, calls=%fused_computation.19 | loop fusion | flops 5760000 | bytes 4609536 | tf_op jit(solution)/shard_map/cos | solution.py:27
  157.3 2.3 fusion.6
  159.9 20.9 %all-gather.1 = bf16[8,2,768]{2,1,0:T(2,128)(2,1)} all-gather(bf16[1,2,768]{2,1,0:T(2,128)(2,1)S(1)} %fusion.24), channel_id=2, replica_groups=mesh['grp'=64,'mem'=8] {'mem'}, dimensions={0}, use_global_device_ids=true | all-gather | bytes 27648 | tf_op jit(solution)/shard_map/all_gather | solution.py:72
  181.2 3.8 cosine_convert_fusion
  185.1 296.0 %all-gather.4.cloned.1.call-done = bf16[512,2,768]{2,1,0:T(2,128)(2,1)} async-done(((bf16[8,2,768]{2,1,0:T(2,128)(2,1)}), bf16[512,2,768]{2,1,0:T(2,128)(2,1)}) %all-gather.4.cloned.1.call-update) | async-done | bytes 1572880 | tf_op jit(solution)/shard_map/all_gather | solution.py:73
  481.1 2.4 fusion.34
  483.5 1.3 copy.16
  484.9 1.3 copy.17
  488.4 1.2 add_convert_fusion
  489.7 1.5 copy.18
  491.2 1.3 subtract_convert_fusion
  492.5 1.4 copy.19
  493.9 3.1 multiply_convert_fusion
  497.0 1.6 copy.20
  498.6 1.9 slice_bitcast_fusion
  (20 shorter events, 4.4 us)
Async XLA Ops:
  6.5 68.6 %copy-start = (f32[8,6030]{1,0:T(8,128)S(1)}, f32[8,6030]{1,0:T(8,128)}, u32[]{:S(2)}) copy-start(f32[8,6030]{1,0:T(8,128)} %param.1) | copy-start | bytes 578884
  6.5 474.5 %all-gather.4.cloned.1.call-start = ((), (), s32[]{:S(2)}) async-start(), calls=%async_computation | async-start | bytes 1597440 | tf_op jit(solution)/shard_map/all_gather | solution.py:73
Sparse Core Ops, SparseCore 0:
  180.9 300.0 all-gather.3
where the time goes:
time: 517 us; the launch traced here: 508 us
  waiting for transfers between devices  296 us (57%)
  local copies, waits for them, and re-layouts  133 us (26%)
  other arithmetic  34 us (7%)
  blocking collectives  20.9 us (4%)
  between operations  14.1 us (3%)
  matrix products  10.2 us (2%)
    all_gather x1, waiting for transfers between devices, on_device(): piece = lax.all_gather(panel, 'grp', axis=0, tiled=True)  296 us
    slice x32, local copies, waits for them, and re-layouts, whiten(): piece = lax.slice(raw_traces, (0, k), (count, k + 2 * total - 1), (1, 2))  119 us
    all_gather x1, blocking collectives, on_device(): panel = lax.all_gather(own_source, 'mem', axis=0, tiled=True)  20.9 us
    add x1, other arithmetic, whiten(): decimated = decimated + filt[k] * piece  20.3 us
  transfers between devices with their start and end apart: 1, of which 1 were waited for; matrix products, arithmetic and copies ran while one was open for 1% of the time, Pallas kernels for 0%

commit v1 on v0

v1 whole, which is shorter than its diff:
```python
import functools
import math

import numpy as np
import jax
import jax.numpy as jnp
from jax import lax
from jax.experimental import pallas as pl
from jax.sharding import PartitionSpec as P

CH_DEV = 8
WINDOWS = 2
WLEN = 1500
NFREQ = 384
TAPS = 32
MAXLAG = 200


def lowpass(taps):
    k = np.arange(taps, dtype=np.float64)
    centre = (taps - 1) / 2.0
    window = 0.5 - 0.5 * np.cos(2.0 * math.pi * (k + 0.5) / taps)
    return 0.5 * np.sinc((k - centre) * 0.5) * window


def forward_table(wlen, nfreq):
    times = np.arange(wlen, dtype=np.int64)
    bins = np.arange(1, nfreq + 1, dtype=np.int64)
    angle = 2.0 * math.pi * ((times[:, None] * bins[None, :]) % wlen) / wlen
    return np.concatenate([np.cos(angle), -np.sin(angle)], axis=1)


def filtered_table(wlen, nfreq, taps):
    filt = lowpass(taps)
    dft = forward_table(wlen, nfreq)
    table = np.zeros((2 * wlen + taps - 2, 2 * nfreq), np.float64)
    for k in range(taps):
        table[k : k + 2 * wlen : 2] += filt[k] * dft
    return table.astype(np.float32)


def inverse_table(wlen, nfreq, maxlag):
    bins = np.arange(1, nfreq + 1, dtype=np.int64)
    shifts = np.arange(2 * maxlag + 1, dtype=np.int64) - maxlag
    phase = np.mod(bins[:, None] * shifts[None, :], wlen).astype(np.float32)
    angle = np.float32(2.0 * math.pi) * phase / np.float32(wlen)
    table = np.concatenate([np.cos(angle), -np.sin(angle)], axis=0).astype(np.float32)
    padded = np.zeros((table.shape[0], -(-table.shape[1] // 128) * 128), np.float32)
    padded[:, : table.shape[1]] = table
    return jnp.asarray(padded).astype(jnp.bfloat16)


def whiten(raw_traces):
    count = raw_traces.shape[0]
    span = 2 * WLEN + TAPS - 2
    windows = jnp.stack(
        [raw_traces[:, w * 2 * WLEN : w * 2 * WLEN + span] for w in range(WINDOWS)], axis=1
    ).reshape(count * WINDOWS, span)
    spec = jnp.dot(
        windows,
        jnp.asarray(filtered_table(WLEN, NFREQ, TAPS)),
        precision=lax.Precision.HIGHEST,
        preferred_element_type=jnp.float32,
    )
    spec_re = spec[:, :NFREQ]
    spec_im = spec[:, NFREQ:]
    power = spec_re * spec_re + spec_im * spec_im
    level = 0.01 * jnp.mean(power, axis=1, keepdims=True)
    factor = 1.0 / jnp.sqrt(power + level + 1e-06)
    white = jnp.concatenate([spec_re * factor, spec_im * factor], axis=1)
    return white.astype(jnp.bfloat16).reshape(count, WINDOWS, 2 * NFREQ)


SRC_BLOCK = 128


def correlate_kernel(scale, recv_ref, src_ref, table_ref, out_ref):
    nf = NFREQ
    src = src_ref[...].astype(jnp.float32)
    s_re0, s_im0 = src[:, 0:nf], src[:, nf : 2 * nf]
    s_re1, s_im1 = src[:, 2 * nf : 3 * nf], src[:, 3 * nf : 4 * nf]
    t_re = table_ref[0:nf, :]
    t_im = table_ref[nf : 2 * nf, :]
    lags = out_ref.shape[2]
    for c in range(out_ref.shape[0]):
        a = recv_ref[c : c + 1, :].astype(jnp.float32)
        a_re0, a_im0 = a[:, 0:nf], a[:, nf : 2 * nf]
        a_re1, a_im1 = a[:, 2 * nf : 3 * nf], a[:, 3 * nf : 4 * nf]
        c_re = (a_re0 * s_re0 + a_im0 * s_im0) + (a_re1 * s_re1 + a_im1 * s_im1)
        c_im = (a_im0 * s_re0 - a_re0 * s_im0) + (a_im1 * s_re1 - a_re1 * s_im1)
        acc = jnp.dot(c_re.astype(jnp.bfloat16), t_re, preferred_element_type=jnp.float32)
        acc = acc + jnp.dot(c_im.astype(jnp.bfloat16), t_im, preferred_element_type=jnp.float32)
        out_ref[c] = (acc[:, :lags] * scale).astype(out_ref.dtype)


def correlate(recv, src, table, lags):
    count, width = recv.shape[0], src.shape[0]
    block = min(SRC_BLOCK, width)
    scale = 1.0 / math.sqrt(WINDOWS * NFREQ)
    flops = 2 * count * width * table.shape[0] * table.shape[1] + 16 * count * width * NFREQ
    bytes_accessed = 2 * (recv.size + src.size + table.size + count * width * lags)
    return pl.pallas_call(
        functools.partial(correlate_kernel, scale),
        grid=(width // block,),
        in_specs=[
            pl.BlockSpec((count, recv.shape[1]), lambda j: (0, 0)),
            pl.BlockSpec((block, src.shape[1]), lambda j: (j, 0)),
            pl.BlockSpec(table.shape, lambda j: (0, 0)),
        ],
        out_specs=pl.BlockSpec((count, block, lags), lambda j: (0, j, 0)),
        out_shape=jax.ShapeDtypeStruct((count, width, lags), jnp.bfloat16),
        cost_estimate=pl.CostEstimate(flops=flops, transcendentals=0, bytes_accessed=bytes_accessed),
    )(recv, src, table)


def gather_sources(own_source):
    axes = ("grp", "mem")
    total = 1
    for name in axes:
        total *= lax.axis_size(name)
    copies = jnp.broadcast_to(own_source, (total,) + own_source.shape[1:])
    return lax.all_to_all(copies, axes, 0, 0, tiled=True)


def on_device(raw_traces):
    white = whiten(raw_traces)
    count = white.shape[0]
    sources = gather_sources(white[:1])
    recv = white.reshape(count, WINDOWS * 2 * NFREQ)
    src = sources.reshape(sources.shape[0], WINDOWS * 2 * NFREQ)
    return correlate(recv, src, inverse_table(WLEN, NFREQ, MAXLAG), 2 * MAXLAG + 1)


def solution(mesh):
    return jax.shard_map(
        on_device,
        mesh=mesh,
        in_specs=(P(("grp", "mem"), None),),
        out_specs=P(("grp", "mem"), None, None),
        check_vma=False,
    )
```

time: 517 us -> 94 us (0.18)
  the two profiles are of different devices: /device:TPU:8 before, /device:TPU:1 now
where the time goes in v1:
time: 94 us; the launch traced here: 93.6 us
  waiting for transfers between devices  43.5 us (46%)
  starting transfers between devices  22.2 us (24%)
  local copies, waits for them, and re-layouts  13.1 us (14%)
  Pallas kernels  7.55 us (8%)
  matrix products  6.99 us (7%)
    all_to_all x1, waiting for transfers between devices, gather_sources(): return lax.all_to_all(copies, axes, 0, 0, tiled=True)  43.5 us
    all_to_all x1, starting transfers between devices, gather_sources(): return lax.all_to_all(copies, axes, 0, 0, tiled=True)  22.2 us
    pallas_call x1, local copies, waits for them, and re-layouts, correlate(): pl.pallas_call(functools.partial(correlate_kernel, scale), grid=(width //...  7.8 us
    pallas_call x1, Pallas kernels, correlate(): pl.pallas_call(functools.partial(correlate_kernel, scale), grid=(width //...  7.55 us
    dot_general x1, matrix products, whiten(): jnp.dot(windows, jnp.asarray(filtered_table(WLEN, NFREQ, TAPS)), precisio...  6.99 us
    broadcast_in_dim x1, local copies, waits for them, and re-layouts, gather_sources(): copies = jnp.broadcast_to(own_source, (total,) + own_source.shape[1:])  1.95 us
  transfers between devices with their start and end apart: 1, of which 1 were waited for; matrix products, arithmetic and copies ran while one was open for 1% of the time, Pallas kernels for 0%

profile of v1, /device:TPU:1, one launch (start us, length us, event | category | flops | bytes accessed | tf_op | source)
XLA Modules:
  0.0 93.6 jit_solution(18441010307031127268)
XLA Ops:
  0.0 1.1 %slice_bitcast_fusion.1 = (f32[8,1,3030]{2,0,1:T(8,128)S(1)}, f32[8,1,3030]{2,0,1:T(8,128)S(1)}) fusion(f32[8,6030]{1,0:T(8,128)} %param.3), kind=kLoop, calls=%fused_computation.2 | loop fusion | bytes 387840 | tf_op jit(solution)/shard_map/stack | solution.py:56
  1.1 0.2 copy.5
  1.2 0.1 reshape.15
  1.4 7.0 %fusion.1 = f32[16,768]{1,0:T(8,128)S(1)} fusion(f32[16,3030]{1,0:T(8,128)S(1)} %reshape.15, f32[3030,768]{1,0:T(8,128)} %constant.14.clone), kind=kOutput, calls=%fused_computation.10 | convolution fusion | flops 446791680 | bytes 9551232 | tf_op jit(solution)/shard_map/dot_general | solution.py:59
  8.4 0.1 fusion
  8.5 0.1 slice_multiply_fusion.1
  8.6 2.0 %broadcast_in_dim.2 = bf16[512,2,768]{2,1,0:T(2,128)(2,1)} broadcast(bf16[2,768]{1,0:T(2,128)(2,1)S(1)} %slice.23), dimensions={1,2} | broadcast | bytes 1575936 | tf_op jit(solution)/shard_map/broadcast_in_dim | solution.py:121
  10.6 22.2 %all-to-all-start = ((bf16[512,2,768]{2,1,0:T(2,128)(2,1)}), bf16[512,2,768]{2,1,0:T(2,128)(2,1)S(1)}, u32[]{:S(2)}, u32[]{:S(2)}) async-start(bf16[512,2,768]{2,1,0:T(2,128)(2,1)} %broadcast_in_dim.2), calls=%async_computation | async-start | bytes 3145728 | tf_op jit(solution)/shard_map/all_to_all | solution.py:122
  32.8 0.6 convert_element_type.11.recv_ref
  33.4 43.5 %all-to-all-done = bf16[512,2,768]{2,1,0:T(2,128)(2,1)S(1)} async-done(((bf16[512,2,768]{2,1,0:T(2,128)(2,1)}), bf16[512,2,768]{2,1,0:T(2,128)(2,1)S(1)}, u32[]{:S(2)}, u32[]{:S(2)}) %all-to-all-start) | async-done | bytes 1572896 | tf_op jit(solution)/shard_map/all_to_all | solution.py:122
  76.8 1.4 %copy.7 = bf16[64,8,2,768]{3,1,2,0:T(8,128)(2,1)} copy(bf16[64,8,2,768]{3,2,1,0:T(2,128)(2,1)S(1)} %bitcast.8) | data formatting | bytes 3145728
  78.2 7.5 %shard_map.37 = bf16[8,512,401]{2,1,0:T(8,128)(2,1)} custom-call(bf16[8,1536]{1,0:T(8,128)(2,1)} %convert_element_type.11.recv_ref, bf16[512,1536]{1,0:T(8,128)(2,1)} %bitcast.9, bf16[768,512]{1,0:T(8,128)(2,1)} %constant.17.table_ref), custom_call_target="tpu_custom_call" | custom-call | flops 3246391296 | bytes 5668864 | tf_op jit(solution)/shard_map/pallas_call | solution.py:102
  85.8 7.8 %copy.6 = bf16[8,512,401]{1,0,2:T(8,128)(2,1)} copy(bf16[8,512,401]{2,1,0:T(8,128)(2,1)} %shard_map.37) | data formatting | bytes 6569984 | tf_op jit(solution)/shard_map/pallas_call | solution.py:102
  (4 shorter events, 0.0 us)
Async XLA Ops:
  10.6 66.3 %all-to-all-start = ((bf16[512,2,768]{2,1,0:T(2,128)(2,1)}), bf16[512,2,768]{2,1,0:T(2,128)(2,1)S(1)}, u32[]{:S(2)}, u32[]{:S(2)}) async-start(bf16[512,2,768]{2,1,0:T(2,128)(2,1)} %broadcast_in_dim.2), calls=%async_computation | async-start | bytes 3145728 | tf_op jit(solution)/shard_map/all_to_all | solution.py:122

commit v2 on v1

--- a/solution.py
+++ b/solution.py
@@ -45,8 +45,8 @@
     phase = np.mod(bins[:, None] * shifts[None, :], wlen).astype(np.float32)
     angle = np.float32(2.0 * math.pi) * phase / np.float32(wlen)
     table = np.concatenate([np.cos(angle), -np.sin(angle)], axis=0).astype(np.float32)
-    padded = np.zeros((table.shape[0], -(-table.shape[1] // 128) * 128), np.float32)
-    padded[:, : table.shape[1]] = table
+    padded = np.zeros((-(-table.shape[1] // 16) * 16, table.shape[0]), np.float32)
+    padded[: table.shape[1]] = table.T
     return jnp.asarray(padded).astype(jnp.bfloat16)
 
 
@@ -59,7 +59,7 @@
     spec = jnp.dot(
         windows,
         jnp.asarray(filtered_table(WLEN, NFREQ, TAPS)),
-        precision=lax.Precision.HIGHEST,
+        precision=lax.Precision.HIGH,
         preferred_element_type=jnp.float32,
     )
     spec_re = spec[:, :NFREQ]
@@ -77,40 +77,40 @@
 def correlate_kernel(scale, recv_ref, src_ref, table_ref, out_ref):
     nf = NFREQ
     src = src_ref[...].astype(jnp.float32)
-    s_re0, s_im0 = src[:, 0:nf], src[:, nf : 2 * nf]
-    s_re1, s_im1 = src[:, 2 * nf : 3 * nf], src[:, 3 * nf : 4 * nf]
-    t_re = table_ref[0:nf, :]
-    t_im = table_ref[nf : 2 * nf, :]
-    lags = out_ref.shape[2]
-    for c in range(out_ref.shape[0]):
-        a = recv_ref[c : c + 1, :].astype(jnp.float32)
-        a_re0, a_im0 = a[:, 0:nf], a[:, nf : 2 * nf]
-        a_re1, a_im1 = a[:, 2 * nf : 3 * nf], a[:, 3 * nf : 4 * nf]
+    s_re0, s_im0 = src[0:nf], src[nf : 2 * nf]
+    s_re1, s_im1 = src[2 * nf : 3 * nf], src[3 * nf : 4 * nf]
+    t_re = table_ref[:, 0:nf]
+    t_im = table_ref[:, nf : 2 * nf]
+    lags = out_ref.shape[0]
+    for c in range(out_ref.shape[1]):
+        a = recv_ref[:, c : c + 1].astype(jnp.float32)
+        a_re0, a_im0 = a[0:nf], a[nf : 2 * nf]
+        a_re1, a_im1 = a[2 * nf : 3 * nf], a[3 * nf : 4 * nf]
         c_re = (a_re0 * s_re0 + a_im0 * s_im0) + (a_re1 * s_re1 + a_im1 * s_im1)
         c_im = (a_im0 * s_re0 - a_re0 * s_im0) + (a_im1 * s_re1 - a_re1 * s_im1)
-        acc = jnp.dot(c_re.astype(jnp.bfloat16), t_re, preferred_element_type=jnp.float32)
-        acc = acc + jnp.dot(c_im.astype(jnp.bfloat16), t_im, preferred_element_type=jnp.float32)
-        out_ref[c] = (acc[:, :lags] * scale).astype(out_ref.dtype)
+        acc = jnp.dot(t_re, c_re.astype(jnp.bfloat16), preferred_element_type=jnp.float32)
+        acc = acc + jnp.dot(t_im, c_im.astype(jnp.bfloat16), preferred_element_type=jnp.float32)
+        out_ref[:, c, :] = (acc[:lags] * scale).astype(out_ref.dtype)
 
 
-def correlate(recv, src, table, lags):
-    count, width = recv.shape[0], src.shape[0]
+def correlate(recv_t, src_t, table_t, lags):
+    count, width = recv_t.shape[1], src_t.shape[1]
     block = min(SRC_BLOCK, width)
     scale = 1.0 / math.sqrt(WINDOWS * NFREQ)
-    flops = 2 * count * width * table.shape[0] * table.shape[1] + 16 * count * width * NFREQ
-    bytes_accessed = 2 * (recv.size + src.size + table.size + count * width * lags)
+    flops = 2 * count * width * table_t.shape[0] * table_t.shape[1] + 16 * count * width * NFREQ
+    bytes_accessed = 2 * (recv_t.size + src_t.size + table_t.size + count * width * lags)
     return pl.pallas_call(
         functools.partial(correlate_kernel, scale),
         grid=(width // block,),
         in_specs=[
-            pl.BlockSpec((count, recv.shape[1]), lambda j: (0, 0)),
-            pl.BlockSpec((block, src.shape[1]), lambda j: (j, 0)),
-            pl.BlockSpec(table.shape, lambda j: (0, 0)),
+            pl.BlockSpec(recv_t.shape, lambda j: (0, 0)),
+            pl.BlockSpec((src_t.shape[0], block), lambda j: (0, j)),
+            pl.BlockSpec(table_t.shape, lambda j: (0, 0)),
         ],
-        out_specs=pl.BlockSpec((count, block, lags), lambda j: (0, j, 0)),
-        out_shape=jax.ShapeDtypeStruct((count, width, lags), jnp.bfloat16),
+        out_specs=pl.BlockSpec((lags, count, block), lambda j: (0, 0, j)),
+        out_shape=jax.ShapeDtypeStruct((lags, count, width), jnp.bfloat16),
         cost_estimate=pl.CostEstimate(flops=flops, transcendentals=0, bytes_accessed=bytes_accessed),
-    )(recv, src, table)
+    )(recv_t, src_t, table_t)
 
 
 def gather_sources(own_source):
@@ -126,9 +126,10 @@
     white = whiten(raw_traces)
     count = white.shape[0]
     sources = gather_sources(white[:1])
-    recv = white.reshape(count, WINDOWS * 2 * NFREQ)
-    src = sources.reshape(sources.shape[0], WINDOWS * 2 * NFREQ)
-    return correlate(recv, src, inverse_table(WLEN, NFREQ, MAXLAG), 2 * MAXLAG + 1)
+    recv_t = white.reshape(count, WINDOWS * 2 * NFREQ).T
+    src_t = sources.reshape(sources.shape[0], WINDOWS * 2 * NFREQ).T
+    lags_first = correlate(recv_t, src_t, inverse_table(WLEN, NFREQ, MAXLAG), 2 * MAXLAG + 1)
+    return jnp.transpose(lags_first, (1, 2, 0))
 
 
 def solution(mesh):

time: 94 us -> 98.2 us (1.045)
  Pallas kernels: 7.55 us -> 18.5 us
  local copies, waits for them, and re-layouts: 13.1 us -> 7.77 us
    pallas_call x1, Pallas kernels: 7.55 us -> 18.5 us  [correlate(): pl.pallas_call(functools.partial(correlate_kernel, scale), grid=(width //...]
    pallas_call x1 -> x0, local copies, waits for them, and re-layouts: 7.8 us -> none  [correlate(): pl.pallas_call(functools.partial(correlate_kernel, scale), grid=(width //...]
    all_to_all x0 -> x1, local copies, waits for them, and re-layouts: none -> 3.53 us  [gather_sources(): return lax.all_to_all(copies, axes, 0, 0, tiled=True)]
    unnamed x1 -> x0, local copies, waits for them, and re-layouts: 1.4 us -> none
where the time goes in v2:
time: 98.2 us; the launch traced here: 97.9 us
  waiting for transfers between devices  43.1 us (44%)
  starting transfers between devices  22.2 us (23%)
  Pallas kernels  18.5 us (19%)
  local copies, waits for them, and re-layouts  7.77 us (8%)
  matrix products  6.04 us (6%)
    all_to_all x1, waiting for transfers between devices, gather_sources(): return lax.all_to_all(copies, axes, 0, 0, tiled=True)  43.1 us
    all_to_all x1, starting transfers between devices, gather_sources(): return lax.all_to_all(copies, axes, 0, 0, tiled=True)  22.2 us
    pallas_call x1, Pallas kernels, correlate(): pl.pallas_call(functools.partial(correlate_kernel, scale), grid=(width //...  18.5 us
    dot_general x1, matrix products, whiten(): jnp.dot(windows, jnp.asarray(filtered_table(WLEN, NFREQ, TAPS)), precisio...  6.04 us
    all_to_all x1, local copies, waits for them, and re-layouts, gather_sources(): return lax.all_to_all(copies, axes, 0, 0, tiled=True)  3.53 us
  transfers between devices with their start and end apart: 1, of which 1 were waited for; matrix products, arithmetic and copies ran while one was open for 1% of the time, Pallas kernels for 0%

profile of v2, /device:TPU:1, one launch (start us, length us, event | category | flops | bytes accessed | tf_op | source)
XLA Modules:
  0.0 97.9 jit_solution(6590745009966887759)
XLA Ops:
  0.0 1.1 %slice_bitcast_fusion.1 = (f32[8,1,3030]{2,0,1:T(8,128)S(1)}, f32[8,1,3030]{2,0,1:T(8,128)S(1)}) fusion(f32[8,6030]{1,0:T(8,128)} %param.3), kind=kLoop, calls=%fused_computation.2 | loop fusion | bytes 387840 | tf_op jit(solution)/shard_map/stack | solution.py:56
  1.1 0.2 copy.6
  1.2 0.1 reshape.15
  1.4 6.0 %fusion.1 = f32[16,768]{1,0:T(8,128)S(1)} fusion(f32[16,3030]{1,0:T(8,128)S(1)} %reshape.15, f32[3030,768]{1,0:T(8,128)} %constant.14.clone), kind=kOutput, calls=%fused_computation.10 | convolution fusion | flops 223395840 | bytes 9551232 | tf_op jit(solution)/shard_map/dot_general | solution.py:59
  7.4 0.1 fusion
  7.6 0.1 slice_multiply_fusion.1
  7.7 2.0 %broadcast_in_dim.2 = bf16[512,2,768]{2,1,0:T(2,128)(2,1)} broadcast(bf16[2,768]{1,0:T(2,128)(2,1)S(1)} %slice.23), dimensions={1,2} | broadcast | bytes 1575936 | tf_op jit(solution)/shard_map/broadcast_in_dim | solution.py:121
  9.6 22.2 %all-to-all-start = ((bf16[512,2,768]{2,1,0:T(2,128)(2,1)}), bf16[512,2,768]{2,1,0:T(2,128)(2,1)S(1)}, u32[]{:S(2)}, u32[]{:S(2)}) async-start(bf16[512,2,768]{2,1,0:T(2,128)(2,1)} %broadcast_in_dim.2), calls=%async_computation | async-start | bytes 3145728 | tf_op jit(solution)/shard_map/all_to_all | solution.py:122
  31.8 0.9 copy.7
  32.7 43.1 %all-to-all-done = bf16[512,2,768]{2,1,0:T(2,128)(2,1)S(1)} async-done(((bf16[512,2,768]{2,1,0:T(2,128)(2,1)}), bf16[512,2,768]{2,1,0:T(2,128)(2,1)S(1)}, u32[]{:S(2)}, u32[]{:S(2)}) %all-to-all-start) | async-done | bytes 1572896 | tf_op jit(solution)/shard_map/all_to_all | solution.py:122
  75.9 3.5 %copy.8 = bf16[512,2,768]{0,2,1:T(8,128)(2,1)} copy(bf16[512,2,768]{2,1,0:T(2,128)(2,1)S(1)} %all-to-all-done) | data formatting | bytes 3145728 | tf_op jit(solution)/shard_map/all_to_all | solution.py:122
  79.4 18.5 %shard_map.37 = bf16[401,8,512]{2,1,0:T(8,128)(2,1)} custom-call(bf16[1536,8]{1,0:T(8,128)(2,1)} %bitcast.12, bf16[1536,512]{1,0:T(8,128)(2,1)} %bitcast.11, bf16[416,768]{1,0:T(8,128)(2,1)} %constant.17.table_ref), custom_call_target="tpu_custom_call" | custom-call | flops 2642411520 | bytes 5521408 | tf_op jit(solution)/shard_map/pallas_call | solution.py:102
  (5 shorter events, 0.0 us)
Async XLA Ops:
  9.6 66.3 %all-to-all-start = ((bf16[512,2,768]{2,1,0:T(2,128)(2,1)}), bf16[512,2,768]{2,1,0:T(2,128)(2,1)S(1)}, u32[]{:S(2)}, u32[]{:S(2)}) async-start(bf16[512,2,768]{2,1,0:T(2,128)(2,1)} %broadcast_in_dim.2), calls=%async_computation | async-start | bytes 3145728 | tf_op jit(solution)/shard_map/all_to_all | solution.py:122

commit v3 on v1

--- a/solution.py
+++ b/solution.py
@@ -81,7 +81,7 @@
     s_re1, s_im1 = src[:, 2 * nf : 3 * nf], src[:, 3 * nf : 4 * nf]
     t_re = table_ref[0:nf, :]
     t_im = table_ref[nf : 2 * nf, :]
-    lags = out_ref.shape[2]
+    lags = out_ref.shape[1]
     for c in range(out_ref.shape[0]):
         a = recv_ref[c : c + 1, :].astype(jnp.float32)
         a_re0, a_im0 = a[:, 0:nf], a[:, nf : 2 * nf]
@@ -90,7 +90,7 @@
         c_im = (a_im0 * s_re0 - a_re0 * s_im0) + (a_im1 * s_re1 - a_re1 * s_im1)
         acc = jnp.dot(c_re.astype(jnp.bfloat16), t_re, preferred_element_type=jnp.float32)
         acc = acc + jnp.dot(c_im.astype(jnp.bfloat16), t_im, preferred_element_type=jnp.float32)
-        out_ref[c] = (acc[:, :lags] * scale).astype(out_ref.dtype)
+        out_ref[c] = (acc.T[:lags] * scale).astype(out_ref.dtype)
 
 
 def correlate(recv, src, table, lags):
@@ -107,8 +107,8 @@
             pl.BlockSpec((block, src.shape[1]), lambda j: (j, 0)),
             pl.BlockSpec(table.shape, lambda j: (0, 0)),
         ],
-        out_specs=pl.BlockSpec((count, block, lags), lambda j: (0, j, 0)),
-        out_shape=jax.ShapeDtypeStruct((count, width, lags), jnp.bfloat16),
+        out_specs=pl.BlockSpec((count, lags, block), lambda j: (0, 0, j)),
+        out_shape=jax.ShapeDtypeStruct((count, lags, width), jnp.bfloat16),
         cost_estimate=pl.CostEstimate(flops=flops, transcendentals=0, bytes_accessed=bytes_accessed),
     )(recv, src, table)
 
@@ -128,7 +128,8 @@
     sources = gather_sources(white[:1])
     recv = white.reshape(count, WINDOWS * 2 * NFREQ)
     src = sources.reshape(sources.shape[0], WINDOWS * 2 * NFREQ)
-    return correlate(recv, src, inverse_table(WLEN, NFREQ, MAXLAG), 2 * MAXLAG + 1)
+    lags_mid = correlate(recv, src, inverse_table(WLEN, NFREQ, MAXLAG), 2 * MAXLAG + 1)
+    return jnp.transpose(lags_mid, (0, 2, 1))
 
 
 def solution(mesh):

time: 94 us -> 91.1 us (0.969)
  local copies, waits for them, and re-layouts: 13.1 us -> 10.1 us
    pallas_call x1 -> x0, local copies, waits for them, and re-layouts: 7.8 us -> none  [correlate(): pl.pallas_call(functools.partial(correlate_kernel, scale), grid=(width //...]
    transpose x0 -> x1, local copies, waits for them, and re-layouts: none -> 4.74 us  [on_device(): return jnp.transpose(lags_mid, (0, 2, 1))]
where the time goes in v3:
time: 91.1 us; the launch traced here: 90.9 us
  waiting for transfers between devices  43.5 us (48%)
  starting transfers between devices  22.2 us (24%)
  local copies, waits for them, and re-layouts  10.1 us (11%)
  Pallas kernels  7.88 us (9%)
  matrix products  6.99 us (8%)
    all_to_all x1, waiting for transfers between devices, gather_sources(): return lax.all_to_all(copies, axes, 0, 0, tiled=True)  43.5 us
    all_to_all x1, starting transfers between devices, gather_sources(): return lax.all_to_all(copies, axes, 0, 0, tiled=True)  22.2 us
    pallas_call x1, Pallas kernels, correlate(): pl.pallas_call(functools.partial(correlate_kernel, scale), grid=(width //...  7.88 us
    dot_general x1, matrix products, whiten(): jnp.dot(windows, jnp.asarray(filtered_table(WLEN, NFREQ, TAPS)), precisio...  6.99 us
    transpose x1, local copies, waits for them, and re-layouts, on_device(): return jnp.transpose(lags_mid, (0, 2, 1))  4.74 us
    broadcast_in_dim x1, local copies, waits for them, and re-layouts, gather_sources(): copies = jnp.broadcast_to(own_source, (total,) + own_source.shape[1:])  1.95 us
  transfers between devices with their start and end apart: 1, of which 1 were waited for; matrix products, arithmetic and copies ran while one was open for 1% of the time, Pallas kernels for 0%

profile of v3, /device:TPU:1, one launch (start us, length us, event | category | flops | bytes accessed | tf_op | source)
XLA Modules:
  0.0 90.9 jit_solution(13120965936631021720)
XLA Ops:
  0.0 1.1 %slice_bitcast_fusion.1 = (f32[8,1,3030]{2,0,1:T(8,128)S(1)}, f32[8,1,3030]{2,0,1:T(8,128)S(1)}) fusion(f32[8,6030]{1,0:T(8,128)} %param.3), kind=kLoop, calls=%fused_computation.2 | loop fusion | bytes 387840 | tf_op jit(solution)/shard_map/stack | solution.py:56
  1.1 0.2 copy.5
  1.2 0.1 reshape.15
  1.4 7.0 %fusion.1 = f32[16,768]{1,0:T(8,128)S(1)} fusion(f32[16,3030]{1,0:T(8,128)S(1)} %reshape.15, f32[3030,768]{1,0:T(8,128)} %constant.14.clone), kind=kOutput, calls=%fused_computation.10 | convolution fusion | flops 446791680 | bytes 9551232 | tf_op jit(solution)/shard_map/dot_general | solution.py:59
  8.4 0.1 fusion
  8.5 0.1 slice_multiply_fusion.1
  8.6 2.0 %broadcast_in_dim.2 = bf16[512,2,768]{2,1,0:T(2,128)(2,1)} broadcast(bf16[2,768]{1,0:T(2,128)(2,1)S(1)} %slice.23), dimensions={1,2} | broadcast | bytes 1575936 | tf_op jit(solution)/shard_map/broadcast_in_dim | solution.py:121
  10.6 22.2 %all-to-all-start = ((bf16[512,2,768]{2,1,0:T(2,128)(2,1)}), bf16[512,2,768]{2,1,0:T(2,128)(2,1)S(1)}, u32[]{:S(2)}, u32[]{:S(2)}) async-start(bf16[512,2,768]{2,1,0:T(2,128)(2,1)} %broadcast_in_dim.2), calls=%async_computation | async-start | bytes 3145728 | tf_op jit(solution)/shard_map/all_to_all | solution.py:122
  32.8 0.6 convert_element_type.11.recv_ref
  33.4 43.5 %all-to-all-done = bf16[512,2,768]{2,1,0:T(2,128)(2,1)S(1)} async-done(((bf16[512,2,768]{2,1,0:T(2,128)(2,1)}), bf16[512,2,768]{2,1,0:T(2,128)(2,1)S(1)}, u32[]{:S(2)}, u32[]{:S(2)}) %all-to-all-start) | async-done | bytes 1572896 | tf_op jit(solution)/shard_map/all_to_all | solution.py:122
  76.8 1.4 %copy.7 = bf16[64,8,2,768]{3,1,2,0:T(8,128)(2,1)} copy(bf16[64,8,2,768]{3,2,1,0:T(2,128)(2,1)S(1)} %bitcast.9) | data formatting | bytes 3145728
  78.2 7.9 %shard_map.37 = bf16[8,401,512]{2,1,0:T(8,128)(2,1)} custom-call(bf16[8,1536]{1,0:T(8,128)(2,1)} %convert_element_type.11.recv_ref, bf16[512,1536]{1,0:T(8,128)(2,1)} %bitcast.11, bf16[768,512]{1,0:T(8,128)(2,1)} %constant.17.table_ref), custom_call_target="tpu_custom_call" | custom-call | flops 3246391296 | bytes 5668864 | tf_op jit(solution)/shard_map/pallas_call | solution.py:102
  86.1 4.7 %copy.6 = bf16[8,512,401]{1,0,2:T(8,128)(2,1)} copy(bf16[8,512,401]{1,2,0:T(8,128)(2,1)} %bitcast.10) | data formatting | bytes 6569984 | tf_op jit(solution)/shard_map/transpose | solution.py:132
  (4 shorter events, 0.0 us)
Async XLA Ops:
  10.6 66.3 %all-to-all-start = ((bf16[512,2,768]{2,1,0:T(2,128)(2,1)}), bf16[512,2,768]{2,1,0:T(2,128)(2,1)S(1)}, u32[]{:S(2)}, u32[]{:S(2)}) async-start(bf16[512,2,768]{2,1,0:T(2,128)(2,1)} %broadcast_in_dim.2), calls=%async_computation | async-start | bytes 3145728 | tf_op jit(solution)/shard_map/all_to_all | solution.py:122

commit v4 on v3

--- a/solution.py
+++ b/solution.py
@@ -79,18 +79,23 @@
     src = src_ref[...].astype(jnp.float32)
     s_re0, s_im0 = src[:, 0:nf], src[:, nf : 2 * nf]
     s_re1, s_im1 = src[:, 2 * nf : 3 * nf], src[:, 3 * nf : 4 * nf]
-    t_re = table_ref[0:nf, :]
-    t_im = table_ref[nf : 2 * nf, :]
-    lags = out_ref.shape[1]
-    for c in range(out_ref.shape[0]):
+    count, lags, block = out_ref.shape
+    parts_re, parts_im = [], []
+    for c in range(count):
         a = recv_ref[c : c + 1, :].astype(jnp.float32)
         a_re0, a_im0 = a[:, 0:nf], a[:, nf : 2 * nf]
         a_re1, a_im1 = a[:, 2 * nf : 3 * nf], a[:, 3 * nf : 4 * nf]
         c_re = (a_re0 * s_re0 + a_im0 * s_im0) + (a_re1 * s_re1 + a_im1 * s_im1)
         c_im = (a_im0 * s_re0 - a_re0 * s_im0) + (a_im1 * s_re1 - a_re1 * s_im1)
-        acc = jnp.dot(c_re.astype(jnp.bfloat16), t_re, preferred_element_type=jnp.float32)
-        acc = acc + jnp.dot(c_im.astype(jnp.bfloat16), t_im, preferred_element_type=jnp.float32)
-        out_ref[c] = (acc.T[:lags] * scale).astype(out_ref.dtype)
+        parts_re.append(c_re.astype(jnp.bfloat16))
+        parts_im.append(c_im.astype(jnp.bfloat16))
+    cross_re = jnp.concatenate(parts_re, axis=0)
+    cross_im = jnp.concatenate(parts_im, axis=0)
+    acc = jnp.dot(cross_re, table_ref[0:nf, :], preferred_element_type=jnp.float32)
+    acc = acc + jnp.dot(cross_im, table_ref[nf : 2 * nf, :], preferred_element_type=jnp.float32)
+    for c in range(count):
+        rows = acc[c * block : (c + 1) * block]
+        out_ref[c] = (rows.T[:lags] * scale).astype(out_ref.dtype)
 
 
 def correlate(recv, src, table, lags):

time: 91.1 us -> 92.1 us (1.011)
  Pallas kernels: 7.88 us -> 8.83 us
    pallas_call x1, Pallas kernels: 7.88 us -> 8.83 us  [correlate(): pl.pallas_call(functools.partial(correlate_kernel, scale), grid=(width //...]
where the time goes in v4:
time: 92.1 us; the launch traced here: 91.8 us
  waiting for transfers between devices  43.5 us (47%)
  starting transfers between devices  22.2 us (24%)
  local copies, waits for them, and re-layouts  10.1 us (11%)
  Pallas kernels  8.83 us (10%)
  matrix products  6.99 us (8%)
    all_to_all x1, waiting for transfers between devices, gather_sources(): return lax.all_to_all(copies, axes, 0, 0, tiled=True)  43.5 us
    all_to_all x1, starting transfers between devices, gather_sources(): return lax.all_to_all(copies, axes, 0, 0, tiled=True)  22.2 us
    pallas_call x1, Pallas kernels, correlate(): pl.pallas_call(functools.partial(correlate_kernel, scale), grid=(width //...  8.83 us
    dot_general x1, matrix products, whiten(): jnp.dot(windows, jnp.asarray(filtered_table(WLEN, NFREQ, TAPS)), precisio...  6.99 us
    transpose x1, local copies, waits for them, and re-layouts, on_device(): return jnp.transpose(lags_mid, (0, 2, 1))  4.74 us
    broadcast_in_dim x1, local copies, waits for them, and re-layouts, gather_sources(): copies = jnp.broadcast_to(own_source, (total,) + own_source.shape[1:])  1.95 us
  transfers between devices with their start and end apart: 1, of which 1 were waited for; matrix products, arithmetic and copies ran while one was open for 1% of the time, Pallas kernels for 0%

profile of v4, /device:TPU:1, one launch (start us, length us, event | category | flops | bytes accessed | tf_op | source)
XLA Modules:
  0.0 91.8 jit_solution(793179846691242608)
XLA Ops:
  0.0 1.1 %slice_bitcast_fusion.1 = (f32[8,1,3030]{2,0,1:T(8,128)S(1)}, f32[8,1,3030]{2,0,1:T(8,128)S(1)}) fusion(f32[8,6030]{1,0:T(8,128)} %param.3), kind=kLoop, calls=%fused_computation.2 | loop fusion | bytes 387840 | tf_op jit(solution)/shard_map/stack | solution.py:56
  1.1 0.2 copy.5
  1.2 0.1 reshape.15
  1.4 7.0 %fusion.1 = f32[16,768]{1,0:T(8,128)S(1)} fusion(f32[16,3030]{1,0:T(8,128)S(1)} %reshape.15, f32[3030,768]{1,0:T(8,128)} %constant.14.clone), kind=kOutput, calls=%fused_computation.10 | convolution fusion | flops 446791680 | bytes 9551232 | tf_op jit(solution)/shard_map/dot_general | solution.py:59
  8.4 0.1 fusion
  8.5 0.1 slice_multiply_fusion.1
  8.6 2.0 %broadcast_in_dim.2 = bf16[512,2,768]{2,1,0:T(2,128)(2,1)} broadcast(bf16[2,768]{1,0:T(2,128)(2,1)S(1)} %slice.23), dimensions={1,2} | broadcast | bytes 1575936 | tf_op jit(solution)/shard_map/broadcast_in_dim | solution.py:126
  10.6 22.2 %all-to-all-start = ((bf16[512,2,768]{2,1,0:T(2,128)(2,1)}), bf16[512,2,768]{2,1,0:T(2,128)(2,1)S(1)}, u32[]{:S(2)}, u32[]{:S(2)}) async-start(bf16[512,2,768]{2,1,0:T(2,128)(2,1)} %broadcast_in_dim.2), calls=%async_computation | async-start | bytes 3145728 | tf_op jit(solution)/shard_map/all_to_all | solution.py:127
  32.8 0.6 convert_element_type.11.recv_ref
  33.4 43.5 %all-to-all-done = bf16[512,2,768]{2,1,0:T(2,128)(2,1)S(1)} async-done(((bf16[512,2,768]{2,1,0:T(2,128)(2,1)}), bf16[512,2,768]{2,1,0:T(2,128)(2,1)S(1)}, u32[]{:S(2)}, u32[]{:S(2)}) %all-to-all-start) | async-done | bytes 1572896 | tf_op jit(solution)/shard_map/all_to_all | solution.py:127
  76.8 1.4 %copy.7 = bf16[64,8,2,768]{3,1,2,0:T(8,128)(2,1)} copy(bf16[64,8,2,768]{3,2,1,0:T(2,128)(2,1)S(1)} %bitcast.9) | data formatting | bytes 3145728
  78.2 8.8 %shard_map.37 = bf16[8,401,512]{2,1,0:T(8,128)(2,1)} custom-call(bf16[8,1536]{1,0:T(8,128)(2,1)} %convert_element_type.11.recv_ref, bf16[512,1536]{1,0:T(8,128)(2,1)} %bitcast.11, bf16[768,512]{1,0:T(8,128)(2,1)} %constant.17.table_ref), custom_call_target="tpu_custom_call" | custom-call | flops 3246391296 | bytes 5668864 | tf_op jit(solution)/shard_map/pallas_call | solution.py:107
  87.1 4.7 %copy.6 = bf16[8,512,401]{1,0,2:T(8,128)(2,1)} copy(bf16[8,512,401]{1,2,0:T(8,128)(2,1)} %bitcast.10) | data formatting | bytes 6569984 | tf_op jit(solution)/shard_map/transpose | solution.py:137
  (4 shorter events, 0.0 us)
Async XLA Ops:
  10.6 66.3 %all-to-all-start = ((bf16[512,2,768]{2,1,0:T(2,128)(2,1)}), bf16[512,2,768]{2,1,0:T(2,128)(2,1)S(1)}, u32[]{:S(2)}, u32[]{:S(2)}) async-start(bf16[512,2,768]{2,1,0:T(2,128)(2,1)} %broadcast_in_dim.2), calls=%async_computation | async-start | bytes 3145728 | tf_op jit(solution)/shard_map/all_to_all | solution.py:127

commit v5 on v3

--- a/solution.py
+++ b/solution.py
@@ -1,6 +1,7 @@
 import functools
 import math
 
+import ml_dtypes
 import numpy as np
 import jax
 import jax.numpy as jnp
@@ -36,7 +37,17 @@
     table = np.zeros((2 * wlen + taps - 2, 2 * nfreq), np.float64)
     for k in range(taps):
         table[k : k + 2 * wlen : 2] += filt[k] * dft
-    return table.astype(np.float32)
+    high = table.astype(np.float32).astype(ml_dtypes.bfloat16)
+    low = (table - high.astype(np.float64)).astype(np.float32).astype(ml_dtypes.bfloat16)
+    return jnp.asarray(high), jnp.asarray(low)
+
+
+def split3(x):
+    high = x.astype(jnp.bfloat16)
+    rest = x - high.astype(jnp.float32)
+    mid = rest.astype(jnp.bfloat16)
+    low = (rest - mid.astype(jnp.float32)).astype(jnp.bfloat16)
+    return high, mid, low
 
 
 def inverse_table(wlen, nfreq, maxlag):
@@ -56,11 +67,15 @@
     windows = jnp.stack(
         [raw_traces[:, w * 2 * WLEN : w * 2 * WLEN + span] for w in range(WINDOWS)], axis=1
     ).reshape(count * WINDOWS, span)
-    spec = jnp.dot(
-        windows,
-        jnp.asarray(filtered_table(WLEN, NFREQ, TAPS)),
-        precision=lax.Precision.HIGHEST,
-        preferred_element_type=jnp.float32,
+    rows = windows.shape[0]
+    t_high, t_low = filtered_table(WLEN, NFREQ, TAPS)
+    w_high, w_mid, w_low = split3(windows)
+    by_high = jnp.dot(
+        jnp.concatenate([w_high, w_mid, w_low], axis=0), t_high, preferred_element_type=jnp.float32
+    )
+    by_low = jnp.dot(jnp.concatenate([w_high, w_mid], axis=0), t_low, preferred_element_type=jnp.float32)
+    spec = (by_high[:rows] + by_low[:rows]) + (
+        (by_high[rows : 2 * rows] + by_low[rows:]) + by_high[2 * rows :]
     )
     spec_re = spec[:, :NFREQ]
     spec_im = spec[:, NFREQ:]

time: 91.1 us -> 88.7 us (0.974)
  matrix products: 6.99 us -> 4.2 us
    dot_general x1 -> x2, matrix products: 6.99 us -> 4.2 us  [the longest x1 3.31 us: whiten(): jnp.dot(jnp.concatenate([w_high, w_mid], axis=0), t_low, preferred_elemen...]
where the time goes in v5:
time: 88.7 us; the launch traced here: 88.5 us
  waiting for transfers between devices  43.5 us (49%)
  starting transfers between devices  22.2 us (25%)
  local copies, waits for them, and re-layouts  10.4 us (12%)
  Pallas kernels  7.87 us (9%)
  matrix products  4.2 us (5%)
    all_to_all x1, waiting for transfers between devices, gather_sources(): return lax.all_to_all(copies, axes, 0, 0, tiled=True)  43.5 us
    all_to_all x1, starting transfers between devices, gather_sources(): return lax.all_to_all(copies, axes, 0, 0, tiled=True)  22.2 us
    pallas_call x1, Pallas kernels, correlate(): pl.pallas_call(functools.partial(correlate_kernel, scale), grid=(width //...  7.87 us
    transpose x1, local copies, waits for them, and re-layouts, on_device(): return jnp.transpose(lags_mid, (0, 2, 1))  4.74 us
    dot_general x1, matrix products, whiten(): jnp.dot(jnp.concatenate([w_high, w_mid], axis=0), t_low, preferred_elemen...  3.31 us
    broadcast_in_dim x1, local copies, waits for them, and re-layouts, gather_sources(): copies = jnp.broadcast_to(own_source, (total,) + own_source.shape[1:])  1.95 us
  transfers between devices with their start and end apart: 1, of which 1 were waited for; matrix products, arithmetic and copies ran while one was open for 1% of the time, Pallas kernels for 0%

profile of v5, /device:TPU:1, one launch (start us, length us, event | category | flops | bytes accessed | tf_op | source)
XLA Modules:
  0.0 88.5 jit_solution(9849616773387244417)
XLA Ops:
  0.0 1.1 %slice_bitcast_fusion.1 = (f32[8,1,3030]{2,0,1:T(8,128)S(1)}, f32[8,1,3030]{2,0,1:T(8,128)S(1)}) fusion(f32[8,6030]{1,0:T(8,128)} %param.4), kind=kLoop, calls=%fused_computation.9 | loop fusion | bytes 387840 | tf_op jit(solution)/shard_map/stack | solution.py:67
  1.1 0.2 copy.6
  1.2 0.1 reshape.15
  1.4 0.0 copy-start
  1.4 3.3 %fusion.1 = f32[32,768]{1,0:T(8,128)S(1)} fusion(bf16[3030,768]{1,0:T(8,128)(2,1)} %constant.17.clone, bf16[16,3030]{1,0:T(8,128)(2,1)S(1)} %get-tuple-element.7, bf16[16,3030]{1,0:T(8,128)(2,1)S(1)} %get-tuple-element.5), kind=kOutput, calls=%fused_computation.6 | convolution fusion | flops 149318400 | bytes 4946304 | tf_op jit(solution)/shard_map/dot_general | solution.py:76
  4.8 0.4 copy-done
  5.1 0.9 %fusion = f32[48,768]{1,0:T(8,128)S(1)} fusion(bf16[3030,768]{1,0:T(8,128)(2,1)S(1)} %copy-done, bf16[16,3030]{1,0:T(8,128)(2,1)S(1)} %get-tuple-element.6, bf16[16,3030]{1,0:T(8,128)(2,1)S(1)} %get-tuple-element.7, bf16[16,3030]{1,0:T(8,128)(2,1)S(1)} %get-tuple-element.5), kind=kOutput, calls=%fused_computation.1 | convolution fusion | flops 224268480 | bytes 5092416 | tf_op jit(solution)/shard_map/dot_general | solution.py:73
  6.0 0.1 fusion.6
  6.2 0.1 slice_multiply_fusion.1
  6.3 2.0 %broadcast_in_dim.2 = bf16[512,2,768]{2,1,0:T(2,128)(2,1)} broadcast(bf16[2,768]{1,0:T(2,128)(2,1)S(1)} %slice.48), dimensions={1,2} | broadcast | bytes 1575936 | tf_op jit(solution)/shard_map/broadcast_in_dim | solution.py:136
  8.2 22.2 %all-to-all-start = ((bf16[512,2,768]{2,1,0:T(2,128)(2,1)}), bf16[512,2,768]{2,1,0:T(2,128)(2,1)S(1)}, u32[]{:S(2)}, u32[]{:S(2)}) async-start(bf16[512,2,768]{2,1,0:T(2,128)(2,1)} %broadcast_in_dim.2), calls=%async_computation | async-start | bytes 3145728 | tf_op jit(solution)/shard_map/all_to_all | solution.py:137
  30.4 0.6 convert_element_type.31.recv_ref
  31.0 43.5 %all-to-all-done = bf16[512,2,768]{2,1,0:T(2,128)(2,1)S(1)} async-done(((bf16[512,2,768]{2,1,0:T(2,128)(2,1)}), bf16[512,2,768]{2,1,0:T(2,128)(2,1)S(1)}, u32[]{:S(2)}, u32[]{:S(2)}) %all-to-all-start) | async-done | bytes 1572896 | tf_op jit(solution)/shard_map/all_to_all | solution.py:137
  74.5 1.4 %copy.8 = bf16[64,8,2,768]{3,1,2,0:T(8,128)(2,1)} copy(bf16[64,8,2,768]{3,2,1,0:T(2,128)(2,1)S(1)} %bitcast.9) | data formatting | bytes 3145728
  75.9 7.9 %shard_map.46 = bf16[8,401,512]{2,1,0:T(8,128)(2,1)} custom-call(bf16[8,1536]{1,0:T(8,128)(2,1)} %convert_element_type.31.recv_ref, bf16[512,1536]{1,0:T(8,128)(2,1)} %bitcast.11, bf16[768,512]{1,0:T(8,128)(2,1)} %constant.20.table_ref), custom_call_target="tpu_custom_call" | custom-call | flops 3246391296 | bytes 5668864 | tf_op jit(solution)/shard_map/pallas_call | solution.py:117
  83.8 4.7 %copy.7 = bf16[8,512,401]{1,0,2:T(8,128)(2,1)} copy(bf16[8,512,401]{1,2,0:T(8,128)(2,1)} %bitcast.10) | data formatting | bytes 6569984 | tf_op jit(solution)/shard_map/transpose | solution.py:147
  (6 shorter events, 0.1 us)
Async XLA Ops:
  1.4 3.7 %copy-start = (bf16[3030,768]{1,0:T(8,128)(2,1)S(1)}, bf16[3030,768]{1,0:T(8,128)(2,1)}, u32[]{:S(2)}) copy-start(bf16[3030,768]{1,0:T(8,128)(2,1)} %constant.16.clone) | copy-start | bytes 13962244
  8.2 66.3 %all-to-all-start = ((bf16[512,2,768]{2,1,0:T(2,128)(2,1)}), bf16[512,2,768]{2,1,0:T(2,128)(2,1)S(1)}, u32[]{:S(2)}, u32[]{:S(2)}) async-start(bf16[512,2,768]{2,1,0:T(2,128)(2,1)} %broadcast_in_dim.2), calls=%async_computation | async-start | bytes 3145728 | tf_op jit(solution)/shard_map/all_to_all | solution.py:137

commit v6 on v5

--- a/solution.py
+++ b/solution.py
@@ -42,12 +42,16 @@
     return jnp.asarray(high), jnp.asarray(low)
 
 
+def to_bf16_grid(x):
+    return lax.reduce_precision(x, exponent_bits=8, mantissa_bits=7)
+
+
 def split3(x):
-    high = x.astype(jnp.bfloat16)
-    rest = x - high.astype(jnp.float32)
-    mid = rest.astype(jnp.bfloat16)
-    low = (rest - mid.astype(jnp.float32)).astype(jnp.bfloat16)
-    return high, mid, low
+    high = to_bf16_grid(x)
+    rest = x - high
+    mid = to_bf16_grid(rest)
+    low = rest - mid
+    return high.astype(jnp.bfloat16), mid.astype(jnp.bfloat16), low.astype(jnp.bfloat16)
 
 
 def inverse_table(wlen, nfreq, maxlag):

time: 88.7 us -> 88.7 us (level)
  no operation moved by 1% of the time
where the time goes in v6:
time: 88.7 us; the launch traced here: 88.5 us
  waiting for transfers between devices  43.5 us (49%)
  starting transfers between devices  22.2 us (25%)
  local copies, waits for them, and re-layouts  10.4 us (12%)
  Pallas kernels  7.87 us (9%)
  matrix products  4.2 us (5%)
    all_to_all x1, waiting for transfers between devices, gather_sources(): return lax.all_to_all(copies, axes, 0, 0, tiled=True)  43.5 us
    all_to_all x1, starting transfers between devices, gather_sources(): return lax.all_to_all(copies, axes, 0, 0, tiled=True)  22.2 us
    pallas_call x1, Pallas kernels, correlate(): pl.pallas_call(functools.partial(correlate_kernel, scale), grid=(width //...  7.87 us
    transpose x1, local copies, waits for them, and re-layouts, on_device(): return jnp.transpose(lags_mid, (0, 2, 1))  4.74 us
    dot_general x1, matrix products, whiten(): jnp.dot(jnp.concatenate([w_high, w_mid], axis=0), t_low, preferred_elemen...  3.31 us
    broadcast_in_dim x1, local copies, waits for them, and re-layouts, gather_sources(): copies = jnp.broadcast_to(own_source, (total,) + own_source.shape[1:])  1.95 us
  transfers between devices with their start and end apart: 1, of which 1 were waited for; matrix products, arithmetic and copies ran while one was open for 1% of the time, Pallas kernels for 0%

profile of v6, /device:TPU:1, one launch (start us, length us, event | category | flops | bytes accessed | tf_op | source)
XLA Modules:
  0.0 88.5 jit_solution(1667340901955704394)
XLA Ops:
  0.0 1.1 %slice_bitcast_fusion.1 = (f32[8,1,3030]{2,0,1:T(8,128)S(1)}, f32[8,1,3030]{2,0,1:T(8,128)S(1)}) fusion(f32[8,6030]{1,0:T(8,128)} %param.4), kind=kLoop, calls=%fused_computation.11 | loop fusion | bytes 387840 | tf_op jit(solution)/shard_map/stack | solution.py:71
  1.1 0.2 copy.6
  1.2 0.1 reshape.15
  1.4 0.0 copy-start
  1.5 3.3 %fusion.2 = f32[32,768]{1,0:T(8,128)S(1)} fusion(bf16[3030,768]{1,0:T(8,128)(2,1)} %constant.17.clone, bf16[16,3030]{1,0:T(8,128)(2,1)S(1)} %get-tuple-element.7, bf16[16,3030]{1,0:T(8,128)(2,1)S(1)} %get-tuple-element.5), kind=kOutput, calls=%fused_computation.9 | convolution fusion | flops 149318400 | bytes 4946304 | tf_op jit(solution)/shard_map/dot_general | solution.py:80
  4.8 0.3 copy-done
  5.1 0.9 %fusion = f32[48,768]{1,0:T(8,128)S(1)} fusion(bf16[3030,768]{1,0:T(8,128)(2,1)S(1)} %copy-done, bf16[16,3030]{1,0:T(8,128)(2,1)S(1)} %get-tuple-element.6, bf16[16,3030]{1,0:T(8,128)(2,1)S(1)} %get-tuple-element.7, bf16[16,3030]{1,0:T(8,128)(2,1)S(1)} %get-tuple-element.5), kind=kOutput, calls=%fused_computation.1 | convolution fusion | flops 224268480 | bytes 5092416 | tf_op jit(solution)/shard_map/dot_general | solution.py:77
  6.0 0.1 fusion.6
  6.2 0.1 slice_multiply_fusion.1
  6.3 2.0 %broadcast_in_dim.2 = bf16[512,2,768]{2,1,0:T(2,128)(2,1)} broadcast(bf16[2,768]{1,0:T(2,128)(2,1)S(1)} %slice.48), dimensions={1,2} | broadcast | bytes 1575936 | tf_op jit(solution)/shard_map/broadcast_in_dim | solution.py:140
  8.2 22.2 %all-to-all-start = ((bf16[512,2,768]{2,1,0:T(2,128)(2,1)}), bf16[512,2,768]{2,1,0:T(2,128)(2,1)S(1)}, u32[]{:S(2)}, u32[]{:S(2)}) async-start(bf16[512,2,768]{2,1,0:T(2,128)(2,1)} %broadcast_in_dim.2), calls=%async_computation | async-start | bytes 3145728 | tf_op jit(solution)/shard_map/all_to_all | solution.py:141
  30.4 0.6 convert_element_type.23.recv_ref
  31.0 43.5 %all-to-all-done = bf16[512,2,768]{2,1,0:T(2,128)(2,1)S(1)} async-done(((bf16[512,2,768]{2,1,0:T(2,128)(2,1)}), bf16[512,2,768]{2,1,0:T(2,128)(2,1)S(1)}, u32[]{:S(2)}, u32[]{:S(2)}) %all-to-all-start) | async-done | bytes 1572896 | tf_op jit(solution)/shard_map/all_to_all | solution.py:141
  74.5 1.4 %copy.8 = bf16[64,8,2,768]{3,1,2,0:T(8,128)(2,1)} copy(bf16[64,8,2,768]{3,2,1,0:T(2,128)(2,1)S(1)} %bitcast.9) | data formatting | bytes 3145728
  75.9 7.9 %shard_map.46 = bf16[8,401,512]{2,1,0:T(8,128)(2,1)} custom-call(bf16[8,1536]{1,0:T(8,128)(2,1)} %convert_element_type.23.recv_ref, bf16[512,1536]{1,0:T(8,128)(2,1)} %bitcast.11, bf16[768,512]{1,0:T(8,128)(2,1)} %constant.20.table_ref), custom_call_target="tpu_custom_call" | custom-call | flops 3246391296 | bytes 5668864 | tf_op jit(solution)/shard_map/pallas_call | solution.py:121
  83.8 4.7 %copy.7 = bf16[8,512,401]{1,0,2:T(8,128)(2,1)} copy(bf16[8,512,401]{1,2,0:T(8,128)(2,1)} %bitcast.10) | data formatting | bytes 6569984 | tf_op jit(solution)/shard_map/transpose | solution.py:151
  (6 shorter events, 0.1 us)
Async XLA Ops:
  1.4 3.7 %copy-start = (bf16[3030,768]{1,0:T(8,128)(2,1)S(1)}, bf16[3030,768]{1,0:T(8,128)(2,1)}, u32[]{:S(2)}) copy-start(bf16[3030,768]{1,0:T(8,128)(2,1)} %constant.16.clone) | copy-start | bytes 13962244
  8.2 66.3 %all-to-all-start = ((bf16[512,2,768]{2,1,0:T(2,128)(2,1)}), bf16[512,2,768]{2,1,0:T(2,128)(2,1)S(1)}, u32[]{:S(2)}, u32[]{:S(2)}) async-start(bf16[512,2,768]{2,1,0:T(2,128)(2,1)} %broadcast_in_dim.2), calls=%async_computation | async-start | bytes 3145728 | tf_op jit(solution)/shard_map/all_to_all | solution.py:141

commit v7 on v6

--- a/solution.py
+++ b/solution.py
@@ -98,6 +98,8 @@
     src = src_ref[...].astype(jnp.float32)
     s_re0, s_im0 = src[:, 0:nf], src[:, nf : 2 * nf]
     s_re1, s_im1 = src[:, 2 * nf : 3 * nf], src[:, 3 * nf : 4 * nf]
+    s_sum0, s_dif0 = s_re0 + s_im0, s_re0 - s_im0
+    s_sum1, s_dif1 = s_re1 + s_im1, s_re1 - s_im1
     t_re = table_ref[0:nf, :]
     t_im = table_ref[nf : 2 * nf, :]
     lags = out_ref.shape[1]
@@ -105,8 +107,10 @@
         a = recv_ref[c : c + 1, :].astype(jnp.float32)
         a_re0, a_im0 = a[:, 0:nf], a[:, nf : 2 * nf]
         a_re1, a_im1 = a[:, 2 * nf : 3 * nf], a[:, 3 * nf : 4 * nf]
-        c_re = (a_re0 * s_re0 + a_im0 * s_im0) + (a_re1 * s_re1 + a_im1 * s_im1)
-        c_im = (a_im0 * s_re0 - a_re0 * s_im0) + (a_im1 * s_re1 - a_re1 * s_im1)
+        k1_0 = s_re0 * (a_re0 + a_im0)
+        k1_1 = s_re1 * (a_re1 + a_im1)
+        c_re = (k1_0 - a_im0 * s_dif0) + (k1_1 - a_im1 * s_dif1)
+        c_im = (k1_0 - a_re0 * s_sum0) + (k1_1 - a_re1 * s_sum1)
         acc = jnp.dot(c_re.astype(jnp.bfloat16), t_re, preferred_element_type=jnp.float32)
         acc = acc + jnp.dot(c_im.astype(jnp.bfloat16), t_im, preferred_element_type=jnp.float32)
         out_ref[c] = (acc.T[:lags] * scale).astype(out_ref.dtype)

time: 88.7 us -> 89 us (level)
  no operation moved by 1% of the time
where the time goes in v7:
time: 89 us; the launch traced here: 88.7 us
  waiting for transfers between devices  43.5 us (49%)
  starting transfers between devices  22.2 us (25%)
  local copies, waits for them, and re-layouts  10.4 us (12%)
  Pallas kernels  8.11 us (9%)
  matrix products  4.2 us (5%)
    all_to_all x1, waiting for transfers between devices, gather_sources(): return lax.all_to_all(copies, axes, 0, 0, tiled=True)  43.5 us
    all_to_all x1, starting transfers between devices, gather_sources(): return lax.all_to_all(copies, axes, 0, 0, tiled=True)  22.2 us
    pallas_call x1, Pallas kernels, correlate(): pl.pallas_call(functools.partial(correlate_kernel, scale), grid=(width //...  8.11 us
    transpose x1, local copies, waits for them, and re-layouts, on_device(): return jnp.transpose(lags_mid, (0, 2, 1))  4.74 us
    dot_general x1, matrix products, whiten(): jnp.dot(jnp.concatenate([w_high, w_mid], axis=0), t_low, preferred_elemen...  3.31 us
    broadcast_in_dim x1, local copies, waits for them, and re-layouts, gather_sources(): copies = jnp.broadcast_to(own_source, (total,) + own_source.shape[1:])  1.95 us
  transfers between devices with their start and end apart: 1, of which 1 were waited for; matrix products, arithmetic and copies ran while one was open for 1% of the time, Pallas kernels for 0%

profile of v7, /device:TPU:1, one launch (start us, length us, event | category | flops | bytes accessed | tf_op | source)
XLA Modules:
  0.0 88.7 jit_solution(12869891481251820398)
XLA Ops:
  0.0 1.1 %slice_bitcast_fusion.1 = (f32[8,1,3030]{2,0,1:T(8,128)S(1)}, f32[8,1,3030]{2,0,1:T(8,128)S(1)}) fusion(f32[8,6030]{1,0:T(8,128)} %param.4), kind=kLoop, calls=%fused_computation.11 | loop fusion | bytes 387840 | tf_op jit(solution)/shard_map/stack | solution.py:71
  1.1 0.2 copy.6
  1.2 0.1 reshape.15
  1.4 0.0 copy-start
  1.5 3.3 %fusion.2 = f32[32,768]{1,0:T(8,128)S(1)} fusion(bf16[3030,768]{1,0:T(8,128)(2,1)} %constant.17.clone, bf16[16,3030]{1,0:T(8,128)(2,1)S(1)} %get-tuple-element.7, bf16[16,3030]{1,0:T(8,128)(2,1)S(1)} %get-tuple-element.5), kind=kOutput, calls=%fused_computation.9 | convolution fusion | flops 149318400 | bytes 4946304 | tf_op jit(solution)/shard_map/dot_general | solution.py:80
  4.8 0.3 copy-done
  5.1 0.9 %fusion = f32[48,768]{1,0:T(8,128)S(1)} fusion(bf16[3030,768]{1,0:T(8,128)(2,1)S(1)} %copy-done, bf16[16,3030]{1,0:T(8,128)(2,1)S(1)} %get-tuple-element.6, bf16[16,3030]{1,0:T(8,128)(2,1)S(1)} %get-tuple-element.7, bf16[16,3030]{1,0:T(8,128)(2,1)S(1)} %get-tuple-element.5), kind=kOutput, calls=%fused_computation.1 | convolution fusion | flops 224268480 | bytes 5092416 | tf_op jit(solution)/shard_map/dot_general | solution.py:77
  6.0 0.1 fusion.6
  6.2 0.1 slice_multiply_fusion.1
  6.3 2.0 %broadcast_in_dim.2 = bf16[512,2,768]{2,1,0:T(2,128)(2,1)} broadcast(bf16[2,768]{1,0:T(2,128)(2,1)S(1)} %slice.48), dimensions={1,2} | broadcast | bytes 1575936 | tf_op jit(solution)/shard_map/broadcast_in_dim | solution.py:144
  8.2 22.2 %all-to-all-start = ((bf16[512,2,768]{2,1,0:T(2,128)(2,1)}), bf16[512,2,768]{2,1,0:T(2,128)(2,1)S(1)}, u32[]{:S(2)}, u32[]{:S(2)}) async-start(bf16[512,2,768]{2,1,0:T(2,128)(2,1)} %broadcast_in_dim.2), calls=%async_computation | async-start | bytes 3145728 | tf_op jit(solution)/shard_map/all_to_all | solution.py:145
  30.4 0.6 convert_element_type.23.recv_ref
  31.0 43.5 %all-to-all-done = bf16[512,2,768]{2,1,0:T(2,128)(2,1)S(1)} async-done(((bf16[512,2,768]{2,1,0:T(2,128)(2,1)}), bf16[512,2,768]{2,1,0:T(2,128)(2,1)S(1)}, u32[]{:S(2)}, u32[]{:S(2)}) %all-to-all-start) | async-done | bytes 1572896 | tf_op jit(solution)/shard_map/all_to_all | solution.py:145
  74.5 1.4 %copy.8 = bf16[64,8,2,768]{3,1,2,0:T(8,128)(2,1)} copy(bf16[64,8,2,768]{3,2,1,0:T(2,128)(2,1)S(1)} %bitcast.9) | data formatting | bytes 3145728
  75.9 8.1 %shard_map.46 = bf16[8,401,512]{2,1,0:T(8,128)(2,1)} custom-call(bf16[8,1536]{1,0:T(8,128)(2,1)} %convert_element_type.23.recv_ref, bf16[512,1536]{1,0:T(8,128)(2,1)} %bitcast.11, bf16[768,512]{1,0:T(8,128)(2,1)} %constant.20.table_ref), custom_call_target="tpu_custom_call" | custom-call | flops 3246391296 | bytes 5668864 | tf_op jit(solution)/shard_map/pallas_call | solution.py:125
  84.0 4.7 %copy.7 = bf16[8,512,401]{1,0,2:T(8,128)(2,1)} copy(bf16[8,512,401]{1,2,0:T(8,128)(2,1)} %bitcast.10) | data formatting | bytes 6569984 | tf_op jit(solution)/shard_map/transpose | solution.py:155
  (6 shorter events, 0.1 us)
Async XLA Ops:
  1.4 3.7 %copy-start = (bf16[3030,768]{1,0:T(8,128)(2,1)S(1)}, bf16[3030,768]{1,0:T(8,128)(2,1)}, u32[]{:S(2)}) copy-start(bf16[3030,768]{1,0:T(8,128)(2,1)} %constant.16.clone) | copy-start | bytes 13962244
  8.2 66.3 %all-to-all-start = ((bf16[512,2,768]{2,1,0:T(2,128)(2,1)}), bf16[512,2,768]{2,1,0:T(2,128)(2,1)S(1)}, u32[]{:S(2)}, u32[]{:S(2)}) async-start(bf16[512,2,768]{2,1,0:T(2,128)(2,1)} %broadcast_in_dim.2), calls=%async_computation | async-start | bytes 3145728 | tf_op jit(solution)/shard_map/all_to_all | solution.py:145

commit v8 on v6

--- a/solution.py
+++ b/solution.py
@@ -95,9 +95,10 @@
 
 def correlate_kernel(scale, recv_ref, src_ref, table_ref, out_ref):
     nf = NFREQ
-    src = src_ref[...].astype(jnp.float32)
-    s_re0, s_im0 = src[:, 0:nf], src[:, nf : 2 * nf]
-    s_re1, s_im1 = src[:, 2 * nf : 3 * nf], src[:, 3 * nf : 4 * nf]
+    s0 = src_ref[:, 0, :].astype(jnp.float32)
+    s1 = src_ref[:, 1, :].astype(jnp.float32)
+    s_re0, s_im0 = s0[:, 0:nf], s0[:, nf : 2 * nf]
+    s_re1, s_im1 = s1[:, 0:nf], s1[:, nf : 2 * nf]
     t_re = table_ref[0:nf, :]
     t_im = table_ref[nf : 2 * nf, :]
     lags = out_ref.shape[1]
@@ -123,7 +124,7 @@
         grid=(width // block,),
         in_specs=[
             pl.BlockSpec((count, recv.shape[1]), lambda j: (0, 0)),
-            pl.BlockSpec((block, src.shape[1]), lambda j: (j, 0)),
+            pl.BlockSpec((block,) + src.shape[1:], lambda j: (j, 0, 0)),
             pl.BlockSpec(table.shape, lambda j: (0, 0)),
         ],
         out_specs=pl.BlockSpec((count, lags, block), lambda j: (0, 0, j)),
@@ -146,7 +147,7 @@
     count = white.shape[0]
     sources = gather_sources(white[:1])
     recv = white.reshape(count, WINDOWS * 2 * NFREQ)
-    src = sources.reshape(sources.shape[0], WINDOWS * 2 * NFREQ)
+    src = sources
     lags_mid = correlate(recv, src, inverse_table(WLEN, NFREQ, MAXLAG), 2 * MAXLAG + 1)
     return jnp.transpose(lags_mid, (0, 2, 1))
 

time: 88.7 us -> 89.6 us (1.010)
  Pallas kernels: 7.87 us -> 9.02 us
    pallas_call x1, Pallas kernels: 7.87 us -> 9.02 us  [correlate(): pl.pallas_call(functools.partial(correlate_kernel, scale), grid=(width //...]
where the time goes in v8:
time: 89.6 us; the launch traced here: 89.4 us
  waiting for transfers between devices  43.5 us (49%)
  starting transfers between devices  22.2 us (25%)
  local copies, waits for them, and re-layouts  10.2 us (11%)
  Pallas kernels  9.02 us (10%)
  matrix products  4.2 us (5%)
    all_to_all x1, waiting for transfers between devices, gather_sources(): return lax.all_to_all(copies, axes, 0, 0, tiled=True)  43.5 us
    all_to_all x1, starting transfers between devices, gather_sources(): return lax.all_to_all(copies, axes, 0, 0, tiled=True)  22.2 us
    pallas_call x1, Pallas kernels, correlate(): pl.pallas_call(functools.partial(correlate_kernel, scale), grid=(width //...  9.02 us
    transpose x1, local copies, waits for them, and re-layouts, on_device(): return jnp.transpose(lags_mid, (0, 2, 1))  4.74 us
    dot_general x1, matrix products, whiten(): jnp.dot(jnp.concatenate([w_high, w_mid], axis=0), t_low, preferred_elemen...  3.31 us
    broadcast_in_dim x1, local copies, waits for them, and re-layouts, gather_sources(): copies = jnp.broadcast_to(own_source, (total,) + own_source.shape[1:])  1.95 us
  transfers between devices with their start and end apart: 1, of which 1 were waited for; matrix products, arithmetic and copies ran while one was open for 1% of the time, Pallas kernels for 0%

profile of v8, /device:TPU:1, one launch (start us, length us, event | category | flops | bytes accessed | tf_op | source)
XLA Modules:
  0.0 89.4 jit_solution(6701551998612686409)
XLA Ops:
  0.0 1.1 %slice_bitcast_fusion.1 = (f32[8,1,3030]{2,0,1:T(8,128)S(1)}, f32[8,1,3030]{2,0,1:T(8,128)S(1)}) fusion(f32[8,6030]{1,0:T(8,128)} %param.4), kind=kLoop, calls=%fused_computation.11 | loop fusion | bytes 387840 | tf_op jit(solution)/shard_map/stack | solution.py:71
  1.1 0.2 copy.6
  1.2 0.1 reshape.12
  1.4 0.0 copy-start
  1.5 3.3 %fusion.2 = f32[32,768]{1,0:T(8,128)S(1)} fusion(bf16[3030,768]{1,0:T(8,128)(2,1)} %constant.17.clone, bf16[16,3030]{1,0:T(8,128)(2,1)S(1)} %get-tuple-element.7, bf16[16,3030]{1,0:T(8,128)(2,1)S(1)} %get-tuple-element.5), kind=kOutput, calls=%fused_computation.9 | convolution fusion | flops 149318400 | bytes 4946304 | tf_op jit(solution)/shard_map/dot_general | solution.py:80
  4.8 0.3 copy-done
  5.1 0.9 fusion
  6.0 0.1 fusion.6
  6.2 0.1 slice_multiply_fusion.1
  6.3 2.0 %broadcast_in_dim.2 = bf16[512,2,768]{2,1,0:T(2,128)(2,1)} broadcast(bf16[2,768]{1,0:T(2,128)(2,1)S(1)} %slice.48), dimensions={1,2} | broadcast | bytes 1575936 | tf_op jit(solution)/shard_map/broadcast_in_dim | solution.py:141
  8.2 22.2 %all-to-all-start = ((bf16[512,2,768]{2,1,0:T(2,128)(2,1)}), bf16[512,2,768]{2,1,0:T(2,128)(2,1)S(1)}, u32[]{:S(2)}, u32[]{:S(2)}) async-start(bf16[512,2,768]{2,1,0:T(2,128)(2,1)} %broadcast_in_dim.2), calls=%async_computation | async-start | bytes 3145728 | tf_op jit(solution)/shard_map/all_to_all | solution.py:142
  30.4 0.6 convert_element_type.23.recv_ref
  31.0 43.5 %all-to-all-done.src_ref = bf16[512,2,768]{2,1,0:T(2,128)(2,1)S(1)} async-done(((bf16[512,2,768]{2,1,0:T(2,128)(2,1)}), bf16[512,2,768]{2,1,0:T(2,128)(2,1)S(1)}, u32[]{:S(2)}, u32[]{:S(2)}) %all-to-all-start) | async-done | bytes 1572896 | tf_op jit(solution)/shard_map/all_to_all | solution.py:142
  74.5 0.0 copy-start.1
  74.5 1.1 %copy-done.1 = bf16[512,2,768]{2,1,0:T(2,128)(2,1)} copy-done((bf16[512,2,768]{2,1,0:T(2,128)(2,1)}, bf16[512,2,768]{2,1,0:T(2,128)(2,1)S(1)}, u32[]{:S(2)}) %copy-start.1) | copy-done | bytes 1572888
  75.6 9.0 %shard_map.46 = bf16[8,401,512]{2,1,0:T(8,128)(2,1)} custom-call(bf16[8,1536]{1,0:T(8,128)(2,1)} %convert_element_type.23.recv_ref, bf16[512,2,768]{2,1,0:T(2,128)(2,1)} %copy-done.1, bf16[768,512]{1,0:T(8,128)(2,1)} %constant.20.table_ref), custom_call_target="tpu_custom_call" | custom-call | flops 3246391296 | bytes 5668864 | tf_op jit(solution)/shard_map/pallas_call | solution.py:122
  84.7 4.7 %copy.7 = bf16[8,512,401]{1,0,2:T(8,128)(2,1)} copy(bf16[8,512,401]{1,2,0:T(8,128)(2,1)} %bitcast.7) | data formatting | bytes 6569984 | tf_op jit(solution)/shard_map/transpose | solution.py:152
  (6 shorter events, 0.1 us)
Async XLA Ops:
  1.4 3.7 %copy-start = (bf16[3030,768]{1,0:T(8,128)(2,1)S(1)}, bf16[3030,768]{1,0:T(8,128)(2,1)}, u32[]{:S(2)}) copy-start(bf16[3030,768]{1,0:T(8,128)(2,1)} %constant.16.clone) | copy-start | bytes 13962244
  8.2 66.3 %all-to-all-start = ((bf16[512,2,768]{2,1,0:T(2,128)(2,1)}), bf16[512,2,768]{2,1,0:T(2,128)(2,1)S(1)}, u32[]{:S(2)}, u32[]{:S(2)}) async-start(bf16[512,2,768]{2,1,0:T(2,128)(2,1)} %broadcast_in_dim.2), calls=%async_computation | async-start | bytes 3145728 | tf_op jit(solution)/shard_map/all_to_all | solution.py:142
  74.5 1.1 %copy-start.1 = (bf16[512,2,768]{2,1,0:T(2,128)(2,1)}, bf16[512,2,768]{2,1,0:T(2,128)(2,1)S(1)}, u32[]{:S(2)}) copy-start(bf16[512,2,768]{2,1,0:T(2,128)(2,1)S(1)} %all-to-all-done.src_ref) | copy-start | bytes 4718596

commit v9 on v6

--- a/solution.py
+++ b/solution.py
@@ -90,7 +90,7 @@
     return white.astype(jnp.bfloat16).reshape(count, WINDOWS, 2 * NFREQ)
 
 
-SRC_BLOCK = 128
+SRC_BLOCK = 256
 
 
 def correlate_kernel(scale, recv_ref, src_ref, table_ref, out_ref):

time: 88.7 us -> 88.6 us (level)
  no operation moved by 1% of the time
where the time goes in v9:
time: 88.6 us; the launch traced here: 88.3 us
  waiting for transfers between devices  43.5 us (49%)
  starting transfers between devices  22.2 us (25%)
  local copies, waits for them, and re-layouts  10.4 us (12%)
  Pallas kernels  7.71 us (9%)
  matrix products  4.2 us (5%)
    all_to_all x1, waiting for transfers between devices, gather_sources(): return lax.all_to_all(copies, axes, 0, 0, tiled=True)  43.5 us
    all_to_all x1, starting transfers between devices, gather_sources(): return lax.all_to_all(copies, axes, 0, 0, tiled=True)  22.2 us
    pallas_call x1, Pallas kernels, correlate(): pl.pallas_call(functools.partial(correlate_kernel, scale), grid=(width //...  7.71 us
    transpose x1, local copies, waits for them, and re-layouts, on_device(): return jnp.transpose(lags_mid, (0, 2, 1))  4.74 us
    dot_general x1, matrix products, whiten(): jnp.dot(jnp.concatenate([w_high, w_mid], axis=0), t_low, preferred_elemen...  3.31 us
    broadcast_in_dim x1, local copies, waits for them, and re-layouts, gather_sources(): copies = jnp.broadcast_to(own_source, (total,) + own_source.shape[1:])  1.95 us
  transfers between devices with their start and end apart: 1, of which 1 were waited for; matrix products, arithmetic and copies ran while one was open for 1% of the time, Pallas kernels for 0%

profile of v9, /device:TPU:1, one launch (start us, length us, event | category | flops | bytes accessed | tf_op | source)
XLA Modules:
  0.0 88.3 jit_solution(16402211206731190106)
XLA Ops:
  0.0 1.1 %slice_bitcast_fusion.1 = (f32[8,1,3030]{2,0,1:T(8,128)S(1)}, f32[8,1,3030]{2,0,1:T(8,128)S(1)}) fusion(f32[8,6030]{1,0:T(8,128)} %param.4), kind=kLoop, calls=%fused_computation.11 | loop fusion | bytes 387840 | tf_op jit(solution)/shard_map/stack | solution.py:71
  1.1 0.2 copy.6
  1.2 0.1 reshape.15
  1.4 0.0 copy-start
  1.5 3.3 %fusion.2 = f32[32,768]{1,0:T(8,128)S(1)} fusion(bf16[3030,768]{1,0:T(8,128)(2,1)} %constant.17.clone, bf16[16,3030]{1,0:T(8,128)(2,1)S(1)} %get-tuple-element.7, bf16[16,3030]{1,0:T(8,128)(2,1)S(1)} %get-tuple-element.5), kind=kOutput, calls=%fused_computation.9 | convolution fusion | flops 149318400 | bytes 4946304 | tf_op jit(solution)/shard_map/dot_general | solution.py:80
  4.8 0.3 copy-done
  5.1 0.9 %fusion = f32[48,768]{1,0:T(8,128)S(1)} fusion(bf16[3030,768]{1,0:T(8,128)(2,1)S(1)} %copy-done, bf16[16,3030]{1,0:T(8,128)(2,1)S(1)} %get-tuple-element.6, bf16[16,3030]{1,0:T(8,128)(2,1)S(1)} %get-tuple-element.7, bf16[16,3030]{1,0:T(8,128)(2,1)S(1)} %get-tuple-element.5), kind=kOutput, calls=%fused_computation.1 | convolution fusion | flops 224268480 | bytes 5092416 | tf_op jit(solution)/shard_map/dot_general | solution.py:77
  6.0 0.1 fusion.6
  6.2 0.1 slice_multiply_fusion.1
  6.3 2.0 %broadcast_in_dim.2 = bf16[512,2,768]{2,1,0:T(2,128)(2,1)} broadcast(bf16[2,768]{1,0:T(2,128)(2,1)S(1)} %slice.48), dimensions={1,2} | broadcast | bytes 1575936 | tf_op jit(solution)/shard_map/broadcast_in_dim | solution.py:140
  8.2 22.2 %all-to-all-start = ((bf16[512,2,768]{2,1,0:T(2,128)(2,1)}), bf16[512,2,768]{2,1,0:T(2,128)(2,1)S(1)}, u32[]{:S(2)}, u32[]{:S(2)}) async-start(bf16[512,2,768]{2,1,0:T(2,128)(2,1)} %broadcast_in_dim.2), calls=%async_computation | async-start | bytes 3145728 | tf_op jit(solution)/shard_map/all_to_all | solution.py:141
  30.4 0.6 convert_element_type.23.recv_ref
  31.0 43.5 %all-to-all-done = bf16[512,2,768]{2,1,0:T(2,128)(2,1)S(1)} async-done(((bf16[512,2,768]{2,1,0:T(2,128)(2,1)}), bf16[512,2,768]{2,1,0:T(2,128)(2,1)S(1)}, u32[]{:S(2)}, u32[]{:S(2)}) %all-to-all-start) | async-done | bytes 1572896 | tf_op jit(solution)/shard_map/all_to_all | solution.py:141
  74.5 1.4 %copy.8 = bf16[64,8,2,768]{3,1,2,0:T(8,128)(2,1)} copy(bf16[64,8,2,768]{3,2,1,0:T(2,128)(2,1)S(1)} %bitcast.9) | data formatting | bytes 3145728
  75.9 7.7 %shard_map.46 = bf16[8,401,512]{2,1,0:T(8,128)(2,1)} custom-call(bf16[8,1536]{1,0:T(8,128)(2,1)} %convert_element_type.23.recv_ref, bf16[512,1536]{1,0:T(8,128)(2,1)} %bitcast.11, bf16[768,512]{1,0:T(8,128)(2,1)} %constant.20.table_ref), custom_call_target="tpu_custom_call" | custom-call | flops 3246391296 | bytes 5668864 | tf_op jit(solution)/shard_map/pallas_call | solution.py:121
  83.6 4.7 %copy.7 = bf16[8,512,401]{1,0,2:T(8,128)(2,1)} copy(bf16[8,512,401]{1,2,0:T(8,128)(2,1)} %bitcast.10) | data formatting | bytes 6569984 | tf_op jit(solution)/shard_map/transpose | solution.py:151
  (6 shorter events, 0.1 us)
Async XLA Ops:
  1.4 3.7 %copy-start = (bf16[3030,768]{1,0:T(8,128)(2,1)S(1)}, bf16[3030,768]{1,0:T(8,128)(2,1)}, u32[]{:S(2)}) copy-start(bf16[3030,768]{1,0:T(8,128)(2,1)} %constant.16.clone) | copy-start | bytes 13962244
  8.2 66.3 %all-to-all-start = ((bf16[512,2,768]{2,1,0:T(2,128)(2,1)}), bf16[512,2,768]{2,1,0:T(2,128)(2,1)S(1)}, u32[]{:S(2)}, u32[]{:S(2)}) async-start(bf16[512,2,768]{2,1,0:T(2,128)(2,1)} %broadcast_in_dim.2), calls=%async_computation | async-start | bytes 3145728 | tf_op jit(solution)/shard_map/all_to_all | solution.py:141

commit v10 on v9

--- a/solution.py
+++ b/solution.py
@@ -100,8 +100,9 @@
     s_re1, s_im1 = src[:, 2 * nf : 3 * nf], src[:, 3 * nf : 4 * nf]
     t_re = table_ref[0:nf, :]
     t_im = table_ref[nf : 2 * nf, :]
-    lags = out_ref.shape[1]
-    for c in range(out_ref.shape[0]):
+    lags = out_ref.shape[0]
+    results = []
+    for c in range(out_ref.shape[1]):
         a = recv_ref[c : c + 1, :].astype(jnp.float32)
         a_re0, a_im0 = a[:, 0:nf], a[:, nf : 2 * nf]
         a_re1, a_im1 = a[:, 2 * nf : 3 * nf], a[:, 3 * nf : 4 * nf]
@@ -109,7 +110,8 @@
         c_im = (a_im0 * s_re0 - a_re0 * s_im0) + (a_im1 * s_re1 - a_re1 * s_im1)
         acc = jnp.dot(c_re.astype(jnp.bfloat16), t_re, preferred_element_type=jnp.float32)
         acc = acc + jnp.dot(c_im.astype(jnp.bfloat16), t_im, preferred_element_type=jnp.float32)
-        out_ref[c] = (acc.T[:lags] * scale).astype(out_ref.dtype)
+        results.append(acc.T[:lags] * scale)
+    out_ref[...] = jnp.stack(results, axis=1).astype(out_ref.dtype)
 
 
 def correlate(recv, src, table, lags):
@@ -126,8 +128,8 @@
             pl.BlockSpec((block, src.shape[1]), lambda j: (j, 0)),
             pl.BlockSpec(table.shape, lambda j: (0, 0)),
         ],
-        out_specs=pl.BlockSpec((count, lags, block), lambda j: (0, 0, j)),
-        out_shape=jax.ShapeDtypeStruct((count, lags, width), jnp.bfloat16),
+        out_specs=pl.BlockSpec((lags, count, block), lambda j: (0, 0, j)),
+        out_shape=jax.ShapeDtypeStruct((lags, count, width), jnp.bfloat16),
         cost_estimate=pl.CostEstimate(flops=flops, transcendentals=0, bytes_accessed=bytes_accessed),
     )(recv, src, table)
 
@@ -148,7 +150,7 @@
     recv = white.reshape(count, WINDOWS * 2 * NFREQ)
     src = sources.reshape(sources.shape[0], WINDOWS * 2 * NFREQ)
     lags_mid = correlate(recv, src, inverse_table(WLEN, NFREQ, MAXLAG), 2 * MAXLAG + 1)
-    return jnp.transpose(lags_mid, (0, 2, 1))
+    return jnp.transpose(lags_mid, (1, 2, 0))
 
 
 def solution(mesh):

time: 88.6 us -> 89.3 us (level)
  Pallas kernels: 7.71 us -> 13.2 us
  local copies, waits for them, and re-layouts: 10.4 us -> 5.69 us
    pallas_call x1, Pallas kernels: 7.71 us -> 13.2 us  [correlate(): pl.pallas_call(functools.partial(correlate_kernel, scale), grid=(width //...]
    transpose x1 -> x0, local copies, waits for them, and re-layouts: 4.74 us -> none  [on_device(): return jnp.transpose(lags_mid, (0, 2, 1))]
where the time goes in v10:
time: 89.3 us; the launch traced here: 89.1 us
  waiting for transfers between devices  43.5 us (49%)
  starting transfers between devices  22.2 us (25%)
  Pallas kernels  13.2 us (15%)
  local copies, waits for them, and re-layouts  5.69 us (6%)
  matrix products  4.2 us (5%)
    all_to_all x1, waiting for transfers between devices, gather_sources(): return lax.all_to_all(copies, axes, 0, 0, tiled=True)  43.5 us
    all_to_all x1, starting transfers between devices, gather_sources(): return lax.all_to_all(copies, axes, 0, 0, tiled=True)  22.2 us
    pallas_call x1, Pallas kernels, correlate(): pl.pallas_call(functools.partial(correlate_kernel, scale), grid=(width //...  13.2 us
    dot_general x1, matrix products, whiten(): jnp.dot(jnp.concatenate([w_high, w_mid], axis=0), t_low, preferred_elemen...  3.31 us
    broadcast_in_dim x1, local copies, waits for them, and re-layouts, gather_sources(): copies = jnp.broadcast_to(own_source, (total,) + own_source.shape[1:])  1.95 us
  transfers between devices with their start and end apart: 1, of which 1 were waited for; matrix products, arithmetic and copies ran while one was open for 1% of the time, Pallas kernels for 0%

profile of v10, /device:TPU:1, one launch (start us, length us, event | category | flops | bytes accessed | tf_op | source)
XLA Modules:
  0.0 89.1 jit_solution(5042996961861178075)
XLA Ops:
  0.0 1.1 %slice_bitcast_fusion.1 = (f32[8,1,3030]{2,0,1:T(8,128)S(1)}, f32[8,1,3030]{2,0,1:T(8,128)S(1)}) fusion(f32[8,6030]{1,0:T(8,128)} %param.4), kind=kLoop, calls=%fused_computation.11 | loop fusion | bytes 387840 | tf_op jit(solution)/shard_map/stack | solution.py:71
  1.1 0.2 copy.5
  1.2 0.1 reshape.15
  1.4 0.0 copy-start
  1.5 3.3 %fusion.2 = f32[32,768]{1,0:T(8,128)S(1)} fusion(bf16[3030,768]{1,0:T(8,128)(2,1)} %constant.17.clone, bf16[16,3030]{1,0:T(8,128)(2,1)S(1)} %get-tuple-element.7, bf16[16,3030]{1,0:T(8,128)(2,1)S(1)} %get-tuple-element.5), kind=kOutput, calls=%fused_computation.9 | convolution fusion | flops 149318400 | bytes 4946304 | tf_op jit(solution)/shard_map/dot_general | solution.py:80
  4.8 0.3 copy-done
  5.1 0.9 fusion
  6.0 0.1 fusion.6
  6.2 0.1 slice_multiply_fusion.1
  6.3 2.0 %broadcast_in_dim.2 = bf16[512,2,768]{2,1,0:T(2,128)(2,1)} broadcast(bf16[2,768]{1,0:T(2,128)(2,1)S(1)} %slice.48), dimensions={1,2} | broadcast | bytes 1575936 | tf_op jit(solution)/shard_map/broadcast_in_dim | solution.py:142
  8.2 22.2 %all-to-all-start = ((bf16[512,2,768]{2,1,0:T(2,128)(2,1)}), bf16[512,2,768]{2,1,0:T(2,128)(2,1)S(1)}, u32[]{:S(2)}, u32[]{:S(2)}) async-start(bf16[512,2,768]{2,1,0:T(2,128)(2,1)} %broadcast_in_dim.2), calls=%async_computation | async-start | bytes 3145728 | tf_op jit(solution)/shard_map/all_to_all | solution.py:143
  30.4 0.6 convert_element_type.23.recv_ref
  31.0 43.5 %all-to-all-done = bf16[512,2,768]{2,1,0:T(2,128)(2,1)S(1)} async-done(((bf16[512,2,768]{2,1,0:T(2,128)(2,1)}), bf16[512,2,768]{2,1,0:T(2,128)(2,1)S(1)}, u32[]{:S(2)}, u32[]{:S(2)}) %all-to-all-start) | async-done | bytes 1572896 | tf_op jit(solution)/shard_map/all_to_all | solution.py:143
  74.5 1.4 %copy.6 = bf16[64,8,2,768]{3,1,2,0:T(8,128)(2,1)} copy(bf16[64,8,2,768]{3,2,1,0:T(2,128)(2,1)S(1)} %bitcast.9) | data formatting | bytes 3145728
  75.9 13.2 %shard_map.46 = bf16[401,8,512]{2,1,0:T(8,128)(2,1)} custom-call(bf16[8,1536]{1,0:T(8,128)(2,1)} %convert_element_type.23.recv_ref, bf16[512,1536]{1,0:T(8,128)(2,1)} %bitcast.10, bf16[768,512]{1,0:T(8,128)(2,1)} %constant.20.table_ref), custom_call_target="tpu_custom_call" | custom-call | flops 3246391296 | bytes 5668864 | tf_op jit(solution)/shard_map/pallas_call | solution.py:123
  (6 shorter events, 0.1 us)
Async XLA Ops:
  1.4 3.7 %copy-start = (bf16[3030,768]{1,0:T(8,128)(2,1)S(1)}, bf16[3030,768]{1,0:T(8,128)(2,1)}, u32[]{:S(2)}) copy-start(bf16[3030,768]{1,0:T(8,128)(2,1)} %constant.16.clone) | copy-start | bytes 13962244
  8.2 66.3 %all-to-all-start = ((bf16[512,2,768]{2,1,0:T(2,128)(2,1)}), bf16[512,2,768]{2,1,0:T(2,128)(2,1)S(1)}, u32[]{:S(2)}, u32[]{:S(2)}) async-start(bf16[512,2,768]{2,1,0:T(2,128)(2,1)} %broadcast_in_dim.2), calls=%async_computation | async-start | bytes 3145728 | tf_op jit(solution)/shard_map/all_to_all | solution.py:143

commit v11 on v9

--- a/solution.py
+++ b/solution.py
@@ -90,7 +90,7 @@
     return white.astype(jnp.bfloat16).reshape(count, WINDOWS, 2 * NFREQ)
 
 
-SRC_BLOCK = 256
+SRC_BLOCK = 512
 
 
 def correlate_kernel(scale, recv_ref, src_ref, table_ref, out_ref):

time: 88.6 us -> 89.1 us (level)
  no operation moved by 1% of the time
where the time goes in v11:
time: 89.1 us; the launch traced here: 88.8 us
  waiting for transfers between devices  43.5 us (49%)
  starting transfers between devices  22.2 us (25%)
  local copies, waits for them, and re-layouts  10.4 us (12%)
  Pallas kernels  8.19 us (9%)
  matrix products  4.2 us (5%)
    all_to_all x1, waiting for transfers between devices, gather_sources(): return lax.all_to_all(copies, axes, 0, 0, tiled=True)  43.5 us
    all_to_all x1, starting transfers between devices, gather_sources(): return lax.all_to_all(copies, axes, 0, 0, tiled=True)  22.2 us
    pallas_call x1, Pallas kernels, correlate(): pl.pallas_call(functools.partial(correlate_kernel, scale), grid=(width //...  8.19 us
    transpose x1, local copies, waits for them, and re-layouts, on_device(): return jnp.transpose(lags_mid, (0, 2, 1))  4.74 us
    dot_general x1, matrix products, whiten(): jnp.dot(jnp.concatenate([w_high, w_mid], axis=0), t_low, preferred_elemen...  3.31 us
    broadcast_in_dim x1, local copies, waits for them, and re-layouts, gather_sources(): copies = jnp.broadcast_to(own_source, (total,) + own_source.shape[1:])  1.95 us
  transfers between devices with their start and end apart: 1, of which 1 were waited for; matrix products, arithmetic and copies ran while one was open for 1% of the time, Pallas kernels for 0%

profile of v11, /device:TPU:1, one launch (start us, length us, event | category | flops | bytes accessed | tf_op | source)
XLA Modules:
  0.0 88.8 jit_solution(14464040621633301854)
XLA Ops:
  0.0 1.1 %slice_bitcast_fusion.1 = (f32[8,1,3030]{2,0,1:T(8,128)S(1)}, f32[8,1,3030]{2,0,1:T(8,128)S(1)}) fusion(f32[8,6030]{1,0:T(8,128)} %param.4), kind=kLoop, calls=%fused_computation.11 | loop fusion | bytes 387840 | tf_op jit(solution)/shard_map/stack | solution.py:71
  1.1 0.2 copy.6
  1.2 0.1 reshape.15
  1.4 0.0 copy-start
  1.5 3.3 %fusion.2 = f32[32,768]{1,0:T(8,128)S(1)} fusion(bf16[3030,768]{1,0:T(8,128)(2,1)} %constant.17.clone, bf16[16,3030]{1,0:T(8,128)(2,1)S(1)} %get-tuple-element.7, bf16[16,3030]{1,0:T(8,128)(2,1)S(1)} %get-tuple-element.5), kind=kOutput, calls=%fused_computation.9 | convolution fusion | flops 149318400 | bytes 4946304 | tf_op jit(solution)/shard_map/dot_general | solution.py:80
  4.8 0.3 copy-done
  5.1 0.9 fusion
  6.0 0.1 fusion.6
  6.2 0.1 slice_multiply_fusion.1
  6.3 2.0 %broadcast_in_dim.2 = bf16[512,2,768]{2,1,0:T(2,128)(2,1)} broadcast(bf16[2,768]{1,0:T(2,128)(2,1)S(1)} %slice.48), dimensions={1,2} | broadcast | bytes 1575936 | tf_op jit(solution)/shard_map/broadcast_in_dim | solution.py:140
  8.2 22.2 %all-to-all-start = ((bf16[512,2,768]{2,1,0:T(2,128)(2,1)}), bf16[512,2,768]{2,1,0:T(2,128)(2,1)S(1)}, u32[]{:S(2)}, u32[]{:S(2)}) async-start(bf16[512,2,768]{2,1,0:T(2,128)(2,1)} %broadcast_in_dim.2), calls=%async_computation | async-start | bytes 3145728 | tf_op jit(solution)/shard_map/all_to_all | solution.py:141
  30.4 0.6 convert_element_type.23.recv_ref
  31.0 43.5 %all-to-all-done = bf16[512,2,768]{2,1,0:T(2,128)(2,1)S(1)} async-done(((bf16[512,2,768]{2,1,0:T(2,128)(2,1)}), bf16[512,2,768]{2,1,0:T(2,128)(2,1)S(1)}, u32[]{:S(2)}, u32[]{:S(2)}) %all-to-all-start) | async-done | bytes 1572896 | tf_op jit(solution)/shard_map/all_to_all | solution.py:141
  74.5 1.4 %copy.8 = bf16[64,8,2,768]{3,1,2,0:T(8,128)(2,1)} copy(bf16[64,8,2,768]{3,2,1,0:T(2,128)(2,1)S(1)} %bitcast.9) | data formatting | bytes 3145728
  75.9 8.2 %shard_map.46 = bf16[8,401,512]{2,1,0:T(8,128)(2,1)} custom-call(bf16[8,1536]{1,0:T(8,128)(2,1)} %convert_element_type.23.recv_ref, bf16[512,1536]{1,0:T(8,128)(2,1)} %bitcast.11, bf16[768,512]{1,0:T(8,128)(2,1)} %constant.20.table_ref), custom_call_target="tpu_custom_call" | custom-call | flops 3246391296 | bytes 5668864 | tf_op jit(solution)/shard_map/pallas_call | solution.py:121
  84.1 4.7 %copy.7 = bf16[8,512,401]{1,0,2:T(8,128)(2,1)} copy(bf16[8,512,401]{1,2,0:T(8,128)(2,1)} %bitcast.10) | data formatting | bytes 6569984 | tf_op jit(solution)/shard_map/transpose | solution.py:151
  (6 shorter events, 0.1 us)
Async XLA Ops:
  1.4 3.7 %copy-start = (bf16[3030,768]{1,0:T(8,128)(2,1)S(1)}, bf16[3030,768]{1,0:T(8,128)(2,1)}, u32[]{:S(2)}) copy-start(bf16[3030,768]{1,0:T(8,128)(2,1)} %constant.16.clone) | copy-start | bytes 13962244
  8.2 66.3 %all-to-all-start = ((bf16[512,2,768]{2,1,0:T(2,128)(2,1)}), bf16[512,2,768]{2,1,0:T(2,128)(2,1)S(1)}, u32[]{:S(2)}, u32[]{:S(2)}) async-start(bf16[512,2,768]{2,1,0:T(2,128)(2,1)} %broadcast_in_dim.2), calls=%async_computation | async-start | bytes 3145728 | tf_op jit(solution)/shard_map/all_to_all | solution.py:141
